TPU v7x, 1024 devices: a whole 4x4x32 slice. The times are simulated.
1024 devices in a mesh: rep: 128 (over z, y_hi, core), fsdp: 8 (over x, y_lo).
Axes of the slice: x: 4, y: 4 (y_hi: 2, y_lo: 2; y = y_hi * 2 + y_lo), z: 32, core: 2. Of those that a mesh axis runs over, the one named last changes fastest.
Arguments:
- tokens: bfloat16 [128, 512, 5120], P('rep'), may hold values from -6 to 6
- cotangent: bfloat16 [128, 512, 13824], P('rep', None, 'fsdp'), may hold values from -0.119628906 to 0.119628906
- adapter_a: float32 [128, 32, 5120], P('rep', None, 'fsdp'), may hold values from -6 to 6
- adapter_b: float32 [128, 32, 13824], P('rep', None, 'fsdp'), may hold values from -6 to 6
- moment_a: float32 [128, 32, 5120], P('rep', None, 'fsdp'), may hold values from -3 to 3
- moment_b: float32 [128, 32, 13824], P('rep', None, 'fsdp'), may hold values from -3 to 3
- step_start: int32 [1], replicated, may hold values from 0 to 63
Outputs:
- final_a: float32 [128, 32, 5120], P('rep', None, 'fsdp')
- final_b: float32 [128, 32, 13824], P('rep', None, 'fsdp')
All inputs are finite; a program needn't handle non-finite values.
Results may differ from a plain program's by a relative error of at most 0.009.
Values may be sent and summed in bfloat16 or wider, within the bound.
No kernel may reach another device: no remote copies, remote signals or barrier semaphores. Data moves between devices by JAX's collectives and lax.ppermute only.
A program may use at most 32 MiB of HBM per device.

v0:
```python
import jax
import jax.numpy as jnp
from jax import lax
from jax.sharding import PartitionSpec as P

STEPS = 3


learn_rate = 0.3
beta_moment = 0.9


def shifted(block, axis, distance):
    devices = range(lax.axis_size(axis))
    route = [((i - distance) % len(devices), i) for i in devices]
    return lax.ppermute(block, axis, route)


def partner_after(values, level, levels):

    def make(bit):

        def moved(field):
            return shifted(field, "rep", 1 << bit)

        return moved

    return lax.switch(level, [make(bit) for bit in range(levels)], values)


def contract_rows(left, right):
    return lax.dot_general(
        left, right, (((1,), (1,)), ((), ())), preferred_element_type=jnp.float32
    )


def contract_tokens(left, right):
    return lax.dot_general(
        left, right, (((0,), (0,)), ((), ())), preferred_element_type=jnp.float32
    )


def shards(tokens, cotangent, adapter_a, adapter_b, moment_a, moment_b, step_start):
    rows = tokens[0]
    cot = cotangent[0]
    factor_a = adapter_a[0]
    factor_b = adapter_b[0]
    moment_da = moment_a[0]
    moment_db = moment_b[0]
    scale = jnp.float32(rows.shape[1]) ** (-0.5)
    own_width = factor_a.shape[1]
    offset = lax.axis_index("fsdp") * own_width
    own_cols = lax.dynamic_slice_in_dim(rows, offset, own_width, 1)
    levels = lax.axis_size("rep").bit_length() - 1
    for step in range(STEPS):
        level = (step_start[0] + step) % levels
        a16 = factor_a.astype(jnp.bfloat16)
        b16 = factor_b.astype(jnp.bfloat16)
        part_v = contract_rows(cot, b16)
        empty = jnp.zeros((rows.shape[0], a16.shape[0]), jnp.float32)
        piece = lax.all_gather(a16[None], "fsdp", axis=2, tiled=True)
        columns = lax.slice_in_dim(rows, 0, piece.shape[2], axis=1)
        total_u = empty + contract_rows(columns, piece[0])
        total_v = lax.psum(part_v.astype(jnp.bfloat16), "fsdp")
        low_u = (total_u * scale).astype(jnp.bfloat16)
        grad_b = contract_tokens(low_u, cot)
        grad_a = contract_tokens(total_v, own_cols) * scale
        moment_da = beta_moment * moment_da + grad_a
        moment_db = beta_moment * moment_db + grad_b
        stepped = jnp.concatenate(
            [factor_a - learn_rate * moment_da, factor_b - learn_rate * moment_db], axis=1
        )
        merged = 0.5 * (stepped + partner_after(stepped, level, levels))
        factor_a = merged[:, :own_width]
        factor_b = merged[:, own_width:]
    return (factor_a[None], factor_b[None])


def solution(mesh):
    in_specs = (
        P("rep", None, None),
        P("rep", None, "fsdp"),
        P("rep", None, "fsdp"),
        P("rep", None, "fsdp"),
        P("rep", None, "fsdp"),
        P("rep", None, "fsdp"),
        P(),
    )
    out_specs = (P("rep", None, "fsdp"), P("rep", None, "fsdp"))
    return jax.shard_map(shards, mesh=mesh, in_specs=in_specs, out_specs=out_specs, check_vma=False)
```

profile of v0, /device:TPU:2, one launch (start us, length us, event | category | flops | bytes accessed | tf_op | source)
XLA Modules:
  0.0 259.4 jit_solution(5351895915167449264)
XLA Ops:
  0.6 0.0 copy-start
  1.4 0.7 copy-done
  2.1 1.6 fusion.23
  3.8 42.4 %psum.21 = bf16[512,32]{1,0:T(8,128)(2,1)S(1)} all-reduce(bf16[512,32]{1,0:T(8,128)(2,1)S(1)} %fusion.23), channel_id=1, replica_groups=mesh['rep'=128,'fsdp'=8] {'fsdp'}, use_global_device_ids=true, to_apply=%region_0.1 | all-reduce | flops 16384 | bytes 65536 | tf_op jit(solution)/shard_map/psum | solution.py:64
  46.2 1.4 bitcast_subtract_fusion.1
  47.6 0.9 convert_element_type.51
  48.5 28.8 %all_gather.9 = bf16[1,32,5120]{2,1,0:T(8,128)(2,1)S(1)} all-gather(bf16[1,32,640]{2,1,0:T(8,128)(2,1)S(1)} %convert_element_type.51), channel_id=1, replica_groups=mesh['rep'=128,'fsdp'=8] {'fsdp'}, dimensions={2}, use_global_device_ids=true | all-gather | bytes 368640 | tf_op jit(solution)/shard_map/all_gather | solution.py:61
  77.3 5.5 %bitcast_subtract_fusion = (f32[32,1728]{1,0:T(8,128)S(1)}, f32[32,1728]{1,0:T(8,128)S(1)}) fusion(f32[1,32,1728]{2,1,0:T(8,128)} %param.31, bf16[1,512,1728]{1,2,0:T(8,128)(2,1)S(1)} %copy-done, bf16[1,512,5120]{2,1,0:T(8,128)(2,1)} %param.28, bf16[1,32,5120]{2,1,0:T(8,128)(2,1)S(1)} %all_gather.9, f32[1,32,1728]{2,1,0:T(8,128)} %param.33), kind=kOutput, calls=%fused_computation.53 | convolution fusion | flops 224649216 | bytes 8224768 | tf_op jit(solution)/shard_map/dot_general | solution.py:38
  82.8 17.0 %conditional.3 = (f32[32,2368]{1,0:T(8,128)}) conditional(s32[]{:T(128)} %clamp.9, f32[32,2368]{1,0:T(8,128)S(1)} %pad_maximum_fusion, f32[32,2368]{1,0:T(8,128)S(1)} %pad_maximum_fusion, f32[32,2368]{1,0:T(8,128)S(1)} %pad_maximum_fusion, f32[32,2368]{1,0:T(8,128)S(1)} %pad_maximum_fusion, ...), branch_computations={%region_1.2_spmd, %region_2.3_spmd, %region_3.4_spmd, %region_4.5_... | conditional | bytes 1212464 | solution.py:28
  82.8 1.9 collective-permute-start.1
  84.7 15.0 %collective-permute-done.1 = f32[32,2368]{1,0:T(8,128)} collective-permute-done((f32[32,2368]{1,0:T(8,128)S(1)}, f32[32,2368]{1,0:T(8,128)}, u32[]{:S(2)}, u32[]{:S(2)}) %collective-permute-start.1) | collective-permute-done | bytes 303136 | tf_op jit(solution)/shard_map/cond/branch_1_fun/ppermute | solution.py:16
  99.8 1.0 add_multiply_fusion.2
  100.8 0.4 fusion.52
  101.2 30.9 %psum.22 = bf16[512,32]{0,1:T(8,128)(2,1)S(1)} all-reduce(bf16[512,32]{0,1:T(8,128)(2,1)S(1)} %fusion.52), channel_id=1, replica_groups=mesh['rep'=128,'fsdp'=8] {'fsdp'}, use_global_device_ids=true, to_apply=%region_8.9 | all-reduce | flops 16384 | bytes 65536 | tf_op jit(solution)/shard_map/psum | solution.py:64
  132.1 1.3 multiply_subtract_fusion.1
  133.4 28.6 %all-gather = bf16[32,5120]{1,0:T(8,128)(2,1)S(1)} all-gather(bf16[32,640]{1,0:T(8,128)(2,1)S(1)} %slice.43), channel_id=2, replica_groups=mesh['rep'=128,'fsdp'=8] {'fsdp'}, dimensions={1}, use_global_device_ids=true | all-gather | bytes 368640 | tf_op jit(solution)/shard_map/all_gather | solution.py:61
  162.0 4.7 %multiply_subtract_fusion = (f32[32,1728]{1,0:T(8,128)S(1)}, f32[32,1728]{1,0:T(8,128)S(1)}) fusion(f32[32,2368]{1,0:T(8,128)S(1)} %add_multiply_fusion.2, bf16[1,512,1728]{1,2,0:T(8,128)(2,1)S(1)} %copy-done, bf16[32,5120]{1,0:T(8,128)(2,1)S(1)} %all-gather, bf16[1,512,5120]{2,1,0:T(8,128)(2,1)} %param.28, f32[32,1728]{1,0:T(8,128)S(1)} %get-tuple-element.48), kind=kOutput, calls=%fused_computation.54 | convolution fusion | flops 224649216 | bytes 8224768 | tf_op jit(solution)/shard_map/dot_general | solution.py:38
  166.8 10.1 %conditional.4 = (f32[32,2368]{1,0:T(8,128)}) conditional(s32[]{:T(128)} %clamp.10, f32[32,2368]{1,0:T(8,128)S(1)} %pad_maximum_fusion.1, f32[32,2368]{1,0:T(8,128)S(1)} %pad_maximum_fusion.1, f32[32,2368]{1,0:T(8,128)S(1)} %pad_maximum_fusion.1, f32[32,2368]{1,0:T(8,128)S(1)} %pad_maximum_fusion.1, ...), branch_computations={%region_9.10_spmd, %region_10.11_spmd, %region_11.12_spmd, %region... | conditional | bytes 1212464 | solution.py:28
  166.8 1.9 collective-permute-start.9
  168.8 8.2 %collective-permute-done.9 = f32[32,2368]{1,0:T(8,128)} collective-permute-done((f32[32,2368]{1,0:T(8,128)S(1)}, f32[32,2368]{1,0:T(8,128)}, u32[]{:S(2)}, u32[]{:S(2)}) %collective-permute-start.9) | collective-permute-done | bytes 303136 | tf_op jit(solution)/shard_map/cond/branch_2_fun/ppermute | solution.py:16
  177.0 1.0 add_multiply_fusion.1
  178.0 0.4 fusion.49
  178.3 30.7 %psum.23 = bf16[512,32]{0,1:T(8,128)(2,1)S(1)} all-reduce(bf16[512,32]{0,1:T(8,128)(2,1)S(1)} %fusion.49), channel_id=1, replica_groups=mesh['rep'=128,'fsdp'=8] {'fsdp'}, use_global_device_ids=true, to_apply=%region_16.17 | all-reduce | flops 16384 | bytes 65536 | tf_op jit(solution)/shard_map/psum | solution.py:64
  209.0 1.3 fusion.28
  210.4 28.6 %all-gather.1 = bf16[32,5120]{1,0:T(8,128)(2,1)S(1)} all-gather(bf16[32,640]{1,0:T(8,128)(2,1)S(1)} %slice.42), channel_id=3, replica_groups=mesh['rep'=128,'fsdp'=8] {'fsdp'}, dimensions={1}, use_global_device_ids=true | all-gather | bytes 368640 | tf_op jit(solution)/shard_map/all_gather | solution.py:61
  238.9 4.7 %fusion.7 = f32[32,1728]{1,0:T(8,128)S(1)} fusion(bf16[1,512,1728]{1,2,0:T(8,128)(2,1)S(1)} %copy-done, bf16[32,5120]{1,0:T(8,128)(2,1)S(1)} %all-gather.1, bf16[1,512,5120]{2,1,0:T(8,128)(2,1)} %param.28, f32[32,1728]{1,0:T(8,128)S(1)} %get-tuple-element.52, f32[32,2368]{1,0:T(8,128)S(1)} %add_multiply_fusion.1), kind=kOutput, calls=%fused_computation.10 | convolution fusion | flops 224649216 | bytes 8003584 | tf_op jit(solution)/shard_map/dot_general | solution.py:38
  243.7 13.3 %conditional.5 = (f32[32,2368]{1,0:T(8,128)}) conditional(s32[]{:T(128)} %clamp.11, f32[32,2368]{1,0:T(8,128)S(1)} %pad_maximum_fusion.2, f32[32,2368]{1,0:T(8,128)S(1)} %pad_maximum_fusion.2, f32[32,2368]{1,0:T(8,128)S(1)} %pad_maximum_fusion.2, f32[32,2368]{1,0:T(8,128)S(1)} %pad_maximum_fusion.2, ...), branch_computations={%region_17.18_spmd, %region_18.19_spmd, %region_19.20_spmd, %regio... | conditional | bytes 1212464 | solution.py:28
  243.7 1.9 collective-permute-start.17
  245.7 11.4 %collective-permute-done.17 = f32[32,2368]{1,0:T(8,128)} collective-permute-done((f32[32,2368]{1,0:T(8,128)S(1)}, f32[32,2368]{1,0:T(8,128)}, u32[]{:S(2)}, u32[]{:S(2)}) %collective-permute-start.17) | collective-permute-done | bytes 303136 | tf_op jit(solution)/shard_map/cond/branch_3_fun/ppermute | solution.py:16
  257.0 1.0 add_multiply_fusion
  258.0 0.7 slice_bitcast_fusion
  258.7 0.6 slice_bitcast_fusion.1
  (5 shorter events, 0.1 us)
Async XLA Ops:
  0.6 1.5 copy-start
  82.8 17.0 %collective-permute-start.1 = (f32[32,2368]{1,0:T(8,128)S(1)}, f32[32,2368]{1,0:T(8,128)}, u32[]{:S(2)}, u32[]{:S(2)}) collective-permute-start(f32[32,2368]{1,0:T(8,128)S(1)} %param.1), channel_id=1, source_target_pairs={{1008,0},{1016,8},{0,16},{8,24},{16,32},{24,40},{32,48},{40,56},{4... | collective-permute-start | bytes 909320 | tf_op jit(solution)/shard_map/cond/branch_1_fun/ppermute | solution.py:16
  166.8 10.1 %collective-permute-start.9 = (f32[32,2368]{1,0:T(8,128)S(1)}, f32[32,2368]{1,0:T(8,128)}, u32[]{:S(2)}, u32[]{:S(2)}) collective-permute-start(f32[32,2368]{1,0:T(8,128)S(1)} %param.9), channel_id=1, source_target_pairs={{992,0},{1000,8},{1008,16},{1016,24},{0,32},{8,40},{16,48},{24,56}... | collective-permute-start | bytes 909320 | tf_op jit(solution)/shard_map/cond/branch_2_fun/ppermute | solution.py:16
  243.7 13.3 %collective-permute-start.17 = (f32[32,2368]{1,0:T(8,128)S(1)}, f32[32,2368]{1,0:T(8,128)}, u32[]{:S(2)}, u32[]{:S(2)}) collective-permute-start(f32[32,2368]{1,0:T(8,128)S(1)} %param.17), channel_id=1, source_target_pairs={{960,0},{968,8},{976,16},{984,24},{992,32},{1000,40},{1008,48},{10... | collective-permute-start | bytes 909320 | tf_op jit(solution)/shard_map/cond/branch_3_fun/ppermute | solution.py:16
where the time goes:
time: 260 us; the launch traced here: 259 us
  blocking collectives  190 us (73%)
  waiting for transfers between devices  34.6 us (13%)
  matrix products  21.3 us (8%)
  starting transfers between devices  5.76 us (2%)
  other arithmetic  3.97 us (2%)
    psum x3, blocking collectives, shards(): total_v = lax.psum(part_v.astype(jnp.bfloat16), 'fsdp')  104 us
    all_gather x3, blocking collectives, shards(): piece = lax.all_gather(a16[None], 'fsdp', axis=2, tiled=True)  86 us
    ppermute x3, waiting for transfers between devices, shifted(): return lax.ppermute(block, axis, route)  34.6 us
    dot_general x6, matrix products, contract_tokens(): lax.dot_general(left, right, (((0,), (0,)), ((), ())), preferred_element_...  18.9 us
    ppermute x3, starting transfers between devices, shifted(): return lax.ppermute(block, axis, route)  5.76 us
  transfers between devices with their start and end apart: 3, of which 3 were waited for; matrix products, arithmetic and copies ran while one was open for 0% of the time, Pallas kernels for 0%

commit v1 on v0

--- a/solution.py
+++ b/solution.py
@@ -28,6 +28,13 @@
     return lax.switch(level, [make(bit) for bit in range(levels)], values)
 
 
+def fsdp_sum(part):
+    total = part
+    for distance in range(1, lax.axis_size("fsdp")):
+        total = total + shifted(part, "fsdp", distance)
+    return total
+
+
 def contract_rows(left, right):
     return lax.dot_general(
         left, right, (((1,), (1,)), ((), ())), preferred_element_type=jnp.float32
@@ -49,6 +56,7 @@
     moment_db = moment_b[0]
     scale = jnp.float32(rows.shape[1]) ** (-0.5)
     own_width = factor_a.shape[1]
+    rank = factor_a.shape[0]
     offset = lax.axis_index("fsdp") * own_width
     own_cols = lax.dynamic_slice_in_dim(rows, offset, own_width, 1)
     levels = lax.axis_size("rep").bit_length() - 1
@@ -56,15 +64,13 @@
         level = (step_start[0] + step) % levels
         a16 = factor_a.astype(jnp.bfloat16)
         b16 = factor_b.astype(jnp.bfloat16)
+        part_u = contract_rows(own_cols, a16)
         part_v = contract_rows(cot, b16)
-        empty = jnp.zeros((rows.shape[0], a16.shape[0]), jnp.float32)
-        piece = lax.all_gather(a16[None], "fsdp", axis=2, tiled=True)
-        columns = lax.slice_in_dim(rows, 0, piece.shape[2], axis=1)
-        total_u = empty + contract_rows(columns, piece[0])
-        total_v = lax.psum(part_v.astype(jnp.bfloat16), "fsdp")
-        low_u = (total_u * scale).astype(jnp.bfloat16)
+        total = fsdp_sum(jnp.concatenate([part_u, part_v], axis=1))
+        low_u = (total[:, :rank] * scale).astype(jnp.bfloat16)
+        low_v = total[:, rank:].astype(jnp.bfloat16)
         grad_b = contract_tokens(low_u, cot)
-        grad_a = contract_tokens(total_v, own_cols) * scale
+        grad_a = contract_tokens(low_v, own_cols) * scale
         moment_da = beta_moment * moment_da + grad_a
         moment_db = beta_moment * moment_db + grad_b
         stepped = jnp.concatenate(

time: 260 us -> 157 us (0.60)
  the two profiles are of different devices: /device:TPU:2 before, /device:TPU:4 now
where the time goes in v1:
time: 157 us; the launch traced here: 156 us
  starting transfers between devices  91.2 us (58%)
  waiting for transfers between devices  41.3 us (26%)
  matrix products  12.2 us (8%)
  other arithmetic  6.53 us (4%)
  local copies, waits for them, and re-layouts  2.82 us (2%)
  between operations  1.78 us (1%)
    ppermute x24, starting transfers between devices, shifted(): return lax.ppermute(block, axis, route)  91.2 us
    ppermute x24, waiting for transfers between devices, shifted(): return lax.ppermute(block, axis, route)  41.3 us
    dot_general x6, matrix products, contract_rows(): lax.dot_general(left, right, (((1,), (1,)), ((), ())), preferred_element_...  6.36 us
    dot_general x6, matrix products, contract_tokens(): lax.dot_general(left, right, (((0,), (0,)), ((), ())), preferred_element_...  5.86 us
  transfers between devices with their start and end apart: 24, of which 8 were waited for; matrix products, arithmetic and copies ran while one was open for 0% of the time, Pallas kernels for 0%

profile of v1, /device:TPU:4, one launch (start us, length us, event | category | flops | bytes accessed | tf_op | source)
XLA Modules:
  0.0 156.0 jit_solution(5887244832070801702)
XLA Ops:
  0.6 0.0 copy-start
  0.7 1.5 copy-done
  2.1 1.4 fusion.9
  3.5 1.4 fusion.29
  4.9 3.5 %collective-permute-start.21 = (f32[512,64]{0,1:T(8,128)S(1)}, f32[512,64]{0,1:T(8,128)S(1)}, u32[]{:S(2)}, u32[]{:S(2)}) collective-permute-start(f32[512,64]{0,1:T(8,128)S(1)} %pad_maximum_fusion.3), channel_id=1, source_target_pairs={{7,0},{0,1},{1,2},{2,3},{3,4},{4,5},{5,6},{6,7},{15,8},{8,9},{9,10... | collective-permute-start | bytes 393224 | tf_op jit(solution)/shard_map/ppermute | solution.py:16
  8.4 3.1 %collective-permute-start.22 = (f32[512,64]{0,1:T(8,128)S(1)}, f32[512,64]{0,1:T(8,128)S(1)}, u32[]{:S(2)}, u32[]{:S(2)}) collective-permute-start(f32[512,64]{0,1:T(8,128)S(1)} %pad_maximum_fusion.3), channel_id=1, source_target_pairs={{6,0},{7,1},{0,2},{1,3},{2,4},{3,5},{4,6},{5,7},{14,8},{15,9},{8,1... | collective-permute-start | bytes 393224 | tf_op jit(solution)/shard_map/ppermute | solution.py:16
  11.6 14.4 %collective-permute-start.23 = (f32[512,64]{0,1:T(8,128)S(1)}, f32[512,64]{0,1:T(8,128)S(1)}, u32[]{:S(2)}, u32[]{:S(2)}) collective-permute-start(f32[512,64]{0,1:T(8,128)S(1)} %pad_maximum_fusion.3), channel_id=1, source_target_pairs={{5,0},{6,1},{7,2},{0,3},{1,4},{2,5},{3,6},{4,7},{13,8},{14,9},{15,... | collective-permute-start | bytes 393224 | tf_op jit(solution)/shard_map/ppermute | solution.py:16
  25.9 1.9 %collective-permute-start.24 = (f32[512,64]{0,1:T(8,128)S(1)}, f32[512,64]{0,1:T(8,128)S(1)}, u32[]{:S(2)}, u32[]{:S(2)}) collective-permute-start(f32[512,64]{0,1:T(8,128)S(1)} %pad_maximum_fusion.3), channel_id=1, source_target_pairs={{4,0},{5,1},{6,2},{7,3},{0,4},{1,5},{2,6},{3,7},{12,8},{13,9},{14,... | collective-permute-start | bytes 393224 | tf_op jit(solution)/shard_map/ppermute | solution.py:16
  27.9 5.4 %collective-permute-start.25 = (f32[512,64]{0,1:T(8,128)S(1)}, f32[512,64]{0,1:T(8,128)S(1)}, u32[]{:S(2)}, u32[]{:S(2)}) collective-permute-start(f32[512,64]{0,1:T(8,128)S(1)} %pad_maximum_fusion.3), channel_id=1, source_target_pairs={{3,0},{4,1},{5,2},{6,3},{7,4},{0,5},{1,6},{2,7},{11,8},{12,9},{13,... | collective-permute-start | bytes 393224 | tf_op jit(solution)/shard_map/ppermute | solution.py:16
  33.3 3.4 %collective-permute-start.26 = (f32[512,64]{0,1:T(8,128)S(1)}, f32[512,64]{0,1:T(8,128)S(1)}, u32[]{:S(2)}, u32[]{:S(2)}) collective-permute-start(f32[512,64]{0,1:T(8,128)S(1)} %pad_maximum_fusion.3), channel_id=1, source_target_pairs={{2,0},{3,1},{4,2},{5,3},{6,4},{7,5},{0,6},{1,7},{10,8},{11,9},{12,... | collective-permute-start | bytes 393224 | tf_op jit(solution)/shard_map/ppermute | solution.py:16
  36.7 0.0 collective-permute-done.22
  36.7 4.5 %collective-permute-start.27 = (f32[512,64]{0,1:T(8,128)S(1)}, f32[512,64]{0,1:T(8,128)}, u32[]{:S(2)}, u32[]{:S(2)}) collective-permute-start(f32[512,64]{0,1:T(8,128)S(1)} %pad_maximum_fusion.3), channel_id=1, source_target_pairs={{1,0},{2,1},{3,2},{4,3},{5,4},{6,5},{7,6},{0,7},{9,8},{10,9},{11,1... | collective-permute-start | bytes 393224 | tf_op jit(solution)/shard_map/ppermute | solution.py:16
  41.9 0.0 copy-start.4
  41.9 0.0 collective-permute-done.23
  41.9 0.0 collective-permute-done.24
  41.9 0.0 collective-permute-done.26
  42.0 2.7 %collective-permute-done.27 = f32[512,64]{0,1:T(8,128)} collective-permute-done((f32[512,64]{0,1:T(8,128)S(1)}, f32[512,64]{0,1:T(8,128)}, u32[]{:S(2)}, u32[]{:S(2)}) %collective-permute-start.27) | collective-permute-done | bytes 131104 | tf_op jit(solution)/shard_map/ppermute | solution.py:16
  44.7 1.0 add_add_fusion.2
  45.7 0.6 bitcast_subtract_fusion
  46.4 1.3 bitcast_subtract_fusion.1
  47.7 12.1 %conditional.3 = (f32[32,2368]{1,0:T(8,128)}) conditional(s32[]{:T(128)} %clamp.9, f32[32,2368]{1,0:T(8,128)S(1)} %pad_maximum_fusion, f32[32,2368]{1,0:T(8,128)S(1)} %pad_maximum_fusion, f32[32,2368]{1,0:T(8,128)S(1)} %pad_maximum_fusion, f32[32,2368]{1,0:T(8,128)S(1)} %pad_maximum_fusion, ...), branch_computations={%region_0.1_spmd, %region_1.2_spmd, %region_2.3_spmd, %region_3.4_... | conditional | bytes 1212464 | solution.py:28
  47.7 1.9 %collective-permute-start = (f32[32,2368]{1,0:T(8,128)S(1)}, f32[32,2368]{1,0:T(8,128)}, u32[]{:S(2)}, u32[]{:S(2)}) collective-permute-start(f32[32,2368]{1,0:T(8,128)S(1)} %param), channel_id=1, source_target_pairs={{1016,0},{0,8},{8,16},{16,24},{24,32},{32,40},{40,48},{48,56},{56,... | collective-permute-start | bytes 909320 | tf_op jit(solution)/shard_map/cond/branch_0_fun/ppermute | solution.py:16
  49.7 10.1 %collective-permute-done = f32[32,2368]{1,0:T(8,128)} collective-permute-done((f32[32,2368]{1,0:T(8,128)S(1)}, f32[32,2368]{1,0:T(8,128)}, u32[]{:S(2)}, u32[]{:S(2)}) %collective-permute-start) | collective-permute-done | bytes 303136 | tf_op jit(solution)/shard_map/cond/branch_0_fun/ppermute | solution.py:16
  59.8 1.0 add_multiply_fusion.2
  60.8 1.4 fusion.26
  62.2 0.4 fusion.16
  62.6 0.7 pad_maximum_fusion.4
  63.3 3.7 %collective-permute-start.28 = (f32[512,64]{0,1:T(8,128)}, f32[512,64]{0,1:T(8,128)S(1)}, u32[]{:S(2)}, u32[]{:S(2)}) collective-permute-start(f32[512,64]{0,1:T(8,128)} %pad_maximum_fusion.4), channel_id=1, source_target_pairs={{7,0},{0,1},{1,2},{2,3},{3,4},{4,5},{5,6},{6,7},{15,8},{8,9},{9,10... | collective-permute-start | bytes 393224 | tf_op jit(solution)/shard_map/ppermute | solution.py:16
  66.9 3.6 %collective-permute-start.29 = (f32[512,64]{0,1:T(8,128)}, f32[512,64]{0,1:T(8,128)S(1)}, u32[]{:S(2)}, u32[]{:S(2)}) collective-permute-start(f32[512,64]{0,1:T(8,128)} %pad_maximum_fusion.4), channel_id=1, source_target_pairs={{6,0},{7,1},{0,2},{1,3},{2,4},{3,5},{4,6},{5,7},{14,8},{15,9},{8,1... | collective-permute-start | bytes 393224 | tf_op jit(solution)/shard_map/ppermute | solution.py:16
  70.5 3.2 %collective-permute-start.30 = (f32[512,64]{0,1:T(8,128)}, f32[512,64]{0,1:T(8,128)S(1)}, u32[]{:S(2)}, u32[]{:S(2)}) collective-permute-start(f32[512,64]{0,1:T(8,128)} %pad_maximum_fusion.4), channel_id=1, source_target_pairs={{5,0},{6,1},{7,2},{0,3},{1,4},{2,5},{3,6},{4,7},{13,8},{14,9},{15,... | collective-permute-start | bytes 393224 | tf_op jit(solution)/shard_map/ppermute | solution.py:16
  73.8 2.8 %collective-permute-start.31 = (f32[512,64]{0,1:T(8,128)}, f32[512,64]{0,1:T(8,128)S(1)}, u32[]{:S(2)}, u32[]{:S(2)}) collective-permute-start(f32[512,64]{0,1:T(8,128)} %pad_maximum_fusion.4), channel_id=1, source_target_pairs={{4,0},{5,1},{6,2},{7,3},{0,4},{1,5},{2,6},{3,7},{12,8},{13,9},{14,... | collective-permute-start | bytes 393224 | tf_op jit(solution)/shard_map/ppermute | solution.py:16
  76.6 6.3 %collective-permute-start.32 = (f32[512,64]{0,1:T(8,128)}, f32[512,64]{0,1:T(8,128)S(1)}, u32[]{:S(2)}, u32[]{:S(2)}) collective-permute-start(f32[512,64]{0,1:T(8,128)} %pad_maximum_fusion.4), channel_id=1, source_target_pairs={{3,0},{4,1},{5,2},{6,3},{7,4},{0,5},{1,6},{2,7},{11,8},{12,9},{13,... | collective-permute-start | bytes 393224 | tf_op jit(solution)/shard_map/ppermute | solution.py:16
  83.0 3.0 %collective-permute-start.33 = (f32[512,64]{0,1:T(8,128)}, f32[512,64]{0,1:T(8,128)S(1)}, u32[]{:S(2)}, u32[]{:S(2)}) collective-permute-start(f32[512,64]{0,1:T(8,128)} %pad_maximum_fusion.4), channel_id=1, source_target_pairs={{2,0},{3,1},{4,2},{5,3},{6,4},{7,5},{0,6},{1,7},{10,8},{11,9},{12,... | collective-permute-start | bytes 393224 | tf_op jit(solution)/shard_map/ppermute | solution.py:16
  86.0 1.9 %collective-permute-start.34 = (f32[512,64]{0,1:T(8,128)}, f32[512,64]{0,1:T(8,128)S(1)}, u32[]{:S(2)}, u32[]{:S(2)}) collective-permute-start(f32[512,64]{0,1:T(8,128)} %pad_maximum_fusion.4), channel_id=1, source_target_pairs={{1,0},{2,1},{3,2},{4,3},{5,4},{6,5},{7,6},{0,7},{9,8},{10,9},{11,1... | collective-permute-start | bytes 393224 | tf_op jit(solution)/shard_map/ppermute | solution.py:16
  88.0 2.1 %collective-permute-done.33 = f32[512,64]{0,1:T(8,128)S(1)} collective-permute-done((f32[512,64]{0,1:T(8,128)}, f32[512,64]{0,1:T(8,128)S(1)}, u32[]{:S(2)}, u32[]{:S(2)}) %collective-permute-start.33) | collective-permute-done | bytes 131104 | tf_op jit(solution)/shard_map/ppermute | solution.py:16
  90.0 3.0 %collective-permute-done.34 = f32[512,64]{0,1:T(8,128)S(1)} collective-permute-done((f32[512,64]{0,1:T(8,128)}, f32[512,64]{0,1:T(8,128)S(1)}, u32[]{:S(2)}, u32[]{:S(2)}) %collective-permute-start.34) | collective-permute-done | bytes 131104 | tf_op jit(solution)/shard_map/ppermute | solution.py:16
  93.1 0.1 add_add_fusion.1
  93.1 1.3 multiply_subtract_fusion.1
  94.5 0.6 multiply_subtract_fusion
  95.1 12.5 %conditional.4 = (f32[32,2368]{1,0:T(8,128)}) conditional(s32[]{:T(128)} %clamp.10, f32[32,2368]{1,0:T(8,128)S(1)} %pad_maximum_fusion.1, f32[32,2368]{1,0:T(8,128)S(1)} %pad_maximum_fusion.1, f32[32,2368]{1,0:T(8,128)S(1)} %pad_maximum_fusion.1, f32[32,2368]{1,0:T(8,128)S(1)} %pad_maximum_fusion.1, ...), branch_computations={%region_7.8_spmd, %region_8.9_spmd, %region_9.10_spmd, %region_10.... | conditional | bytes 1212464 | solution.py:28
  95.2 1.9 %collective-permute-start.8 = (f32[32,2368]{1,0:T(8,128)S(1)}, f32[32,2368]{1,0:T(8,128)}, u32[]{:S(2)}, u32[]{:S(2)}) collective-permute-start(f32[32,2368]{1,0:T(8,128)S(1)} %param.8), channel_id=1, source_target_pairs={{1008,0},{1016,8},{0,16},{8,24},{16,32},{24,40},{32,48},{40,56},{4... | collective-permute-start | bytes 909320 | tf_op jit(solution)/shard_map/cond/branch_1_fun/ppermute | solution.py:16
  97.1 10.6 %collective-permute-done.8 = f32[32,2368]{1,0:T(8,128)} collective-permute-done((f32[32,2368]{1,0:T(8,128)S(1)}, f32[32,2368]{1,0:T(8,128)}, u32[]{:S(2)}, u32[]{:S(2)}) %collective-permute-start.8) | collective-permute-done | bytes 303136 | tf_op jit(solution)/shard_map/cond/branch_1_fun/ppermute | solution.py:16
  107.7 1.0 add_multiply_fusion.1
  108.7 1.4 fusion.23
  110.1 0.4 fusion.19
  110.5 0.7 pad_maximum_fusion.5
  111.2 2.5 %collective-permute-start.35 = (f32[512,64]{0,1:T(8,128)}, f32[512,64]{0,1:T(8,128)S(1)}, u32[]{:S(2)}, u32[]{:S(2)}) collective-permute-start(f32[512,64]{0,1:T(8,128)} %pad_maximum_fusion.5), channel_id=1, source_target_pairs={{7,0},{0,1},{1,2},{2,3},{3,4},{4,5},{5,6},{6,7},{15,8},{8,9},{9,10... | collective-permute-start | bytes 393224 | tf_op jit(solution)/shard_map/ppermute | solution.py:16
  113.7 3.8 %collective-permute-start.36 = (f32[512,64]{0,1:T(8,128)}, f32[512,64]{0,1:T(8,128)S(1)}, u32[]{:S(2)}, u32[]{:S(2)}) collective-permute-start(f32[512,64]{0,1:T(8,128)} %pad_maximum_fusion.5), channel_id=1, source_target_pairs={{6,0},{7,1},{0,2},{1,3},{2,4},{3,5},{4,6},{5,7},{14,8},{15,9},{8,1... | collective-permute-start | bytes 393224 | tf_op jit(solution)/shard_map/ppermute | solution.py:16
  117.5 3.7 %collective-permute-start.37 = (f32[512,64]{0,1:T(8,128)}, f32[512,64]{0,1:T(8,128)S(1)}, u32[]{:S(2)}, u32[]{:S(2)}) collective-permute-start(f32[512,64]{0,1:T(8,128)} %pad_maximum_fusion.5), channel_id=1, source_target_pairs={{5,0},{6,1},{7,2},{0,3},{1,4},{2,5},{3,6},{4,7},{13,8},{14,9},{15,... | collective-permute-start | bytes 393224 | tf_op jit(solution)/shard_map/ppermute | solution.py:16
  121.2 2.9 %collective-permute-start.38 = (f32[512,64]{0,1:T(8,128)}, f32[512,64]{0,1:T(8,128)S(1)}, u32[]{:S(2)}, u32[]{:S(2)}) collective-permute-start(f32[512,64]{0,1:T(8,128)} %pad_maximum_fusion.5), channel_id=1, source_target_pairs={{4,0},{5,1},{6,2},{7,3},{0,4},{1,5},{2,6},{3,7},{12,8},{13,9},{14,... | collective-permute-start | bytes 393224 | tf_op jit(solution)/shard_map/ppermute | solution.py:16
  124.1 4.6 %collective-permute-start.39 = (f32[512,64]{0,1:T(8,128)}, f32[512,64]{0,1:T(8,128)S(1)}, u32[]{:S(2)}, u32[]{:S(2)}) collective-permute-start(f32[512,64]{0,1:T(8,128)} %pad_maximum_fusion.5), channel_id=1, source_target_pairs={{3,0},{4,1},{5,2},{6,3},{7,4},{0,5},{1,6},{2,7},{11,8},{12,9},{13,... | collective-permute-start | bytes 393224 | tf_op jit(solution)/shard_map/ppermute | solution.py:16
  128.8 4.5 %collective-permute-start.40 = (f32[512,64]{0,1:T(8,128)}, f32[512,64]{0,1:T(8,128)S(1)}, u32[]{:S(2)}, u32[]{:S(2)}) collective-permute-start(f32[512,64]{0,1:T(8,128)} %pad_maximum_fusion.5), channel_id=1, source_target_pairs={{2,0},{3,1},{4,2},{5,3},{6,4},{7,5},{0,6},{1,7},{10,8},{11,9},{12,... | collective-permute-start | bytes 393224 | tf_op jit(solution)/shard_map/ppermute | solution.py:16
  133.3 2.5 %collective-permute-start.41 = (f32[512,64]{0,1:T(8,128)}, f32[512,64]{0,1:T(8,128)}, u32[]{:S(2)}, u32[]{:S(2)}) collective-permute-start(f32[512,64]{0,1:T(8,128)} %pad_maximum_fusion.5), channel_id=1, source_target_pairs={{1,0},{2,1},{3,2},{4,3},{5,4},{6,5},{7,6},{0,7},{9,8},{10,9},{11,1... | collective-permute-start | bytes 393224 | tf_op jit(solution)/shard_map/ppermute | solution.py:16
  135.9 0.2 collective-permute-done.40
  136.1 4.4 %collective-permute-done.41 = f32[512,64]{0,1:T(8,128)} collective-permute-done((f32[512,64]{0,1:T(8,128)}, f32[512,64]{0,1:T(8,128)}, u32[]{:S(2)}, u32[]{:S(2)}) %collective-permute-start.41) | collective-permute-done | bytes 131104 | tf_op jit(solution)/shard_map/ppermute | solution.py:16
  140.5 1.0 add_add_fusion
  141.5 1.3 fusion.13
  142.8 0.6 fusion.1
  143.5 10.1 %conditional.5 = (f32[32,2368]{1,0:T(8,128)}) conditional(s32[]{:T(128)} %clamp.11, f32[32,2368]{1,0:T(8,128)S(1)} %pad_maximum_fusion.2, f32[32,2368]{1,0:T(8,128)S(1)} %pad_maximum_fusion.2, f32[32,2368]{1,0:T(8,128)S(1)} %pad_maximum_fusion.2, f32[32,2368]{1,0:T(8,128)S(1)} %pad_maximum_fusion.2, ...), branch_computations={%region_14.15_spmd, %region_15.16_spmd, %region_16.17_spmd, %regio... | conditional | bytes 1212464 | solution.py:28
  143.5 1.9 %collective-permute-start.16 = (f32[32,2368]{1,0:T(8,128)S(1)}, f32[32,2368]{1,0:T(8,128)}, u32[]{:S(2)}, u32[]{:S(2)}) collective-permute-start(f32[32,2368]{1,0:T(8,128)S(1)} %param.16), channel_id=1, source_target_pairs={{992,0},{1000,8},{1008,16},{1016,24},{0,32},{8,40},{16,48},{24,56}... | collective-permute-start | bytes 909320 | tf_op jit(solution)/shard_map/cond/branch_2_fun/ppermute | solution.py:16
  145.4 8.2 %collective-permute-done.16 = f32[32,2368]{1,0:T(8,128)} collective-permute-done((f32[32,2368]{1,0:T(8,128)S(1)}, f32[32,2368]{1,0:T(8,128)}, u32[]{:S(2)}, u32[]{:S(2)}) %collective-permute-start.16) | collective-permute-done | bytes 303136 | tf_op jit(solution)/shard_map/cond/branch_2_fun/ppermute | solution.py:16
  153.6 1.0 add_multiply_fusion
  154.6 0.7 slice_bitcast_fusion
  155.3 0.6 slice_bitcast_fusion.1
  (23 shorter events, 0.1 us)
Async XLA Ops:
  0.6 1.5 copy-start
  0.6 2.9 %copy-start.2 = (f32[1,32,640]{2,1,0:T(8,128)S(1)}, f32[1,32,640]{2,1,0:T(8,128)}, u32[]{:S(2)}) copy-start(f32[1,32,640]{2,1,0:T(8,128)} %param.30) | copy-start | bytes 245764
  2.1 43.6 %copy-start.1 = (f32[1,32,1728]{2,1,0:T(8,128)S(1)}, f32[1,32,1728]{2,1,0:T(8,128)}, u32[]{:S(2)}) copy-start(f32[1,32,1728]{2,1,0:T(8,128)} %param.31) | copy-start | bytes 663556
  2.1 43.6 %copy-start.3 = (f32[1,32,1728]{2,1,0:T(8,128)S(1)}, f32[1,32,1728]{2,1,0:T(8,128)}, u32[]{:S(2)}) copy-start(f32[1,32,1728]{2,1,0:T(8,128)} %param.33) | copy-start | bytes 663556
  4.9 28.4 %collective-permute-start.21 = (f32[512,64]{0,1:T(8,128)S(1)}, f32[512,64]{0,1:T(8,128)S(1)}, u32[]{:S(2)}, u32[]{:S(2)}) collective-permute-start(f32[512,64]{0,1:T(8,128)S(1)} %pad_maximum_fusion.3), channel_id=1, source_target_pairs={{7,0},{0,1},{1,2},{2,3},{3,4},{4,5},{5,6},{6,7},{15,8},{8,9},{9,10... | collective-permute-start | bytes 393224 | tf_op jit(solution)/shard_map/ppermute | solution.py:16
  8.4 28.2 %collective-permute-start.22 = (f32[512,64]{0,1:T(8,128)S(1)}, f32[512,64]{0,1:T(8,128)S(1)}, u32[]{:S(2)}, u32[]{:S(2)}) collective-permute-start(f32[512,64]{0,1:T(8,128)S(1)} %pad_maximum_fusion.3), channel_id=1, source_target_pairs={{6,0},{7,1},{0,2},{1,3},{2,4},{3,5},{4,6},{5,7},{14,8},{15,9},{8,1... | collective-permute-start | bytes 393224 | tf_op jit(solution)/shard_map/ppermute | solution.py:16
  11.6 30.4 %collective-permute-start.23 = (f32[512,64]{0,1:T(8,128)S(1)}, f32[512,64]{0,1:T(8,128)S(1)}, u32[]{:S(2)}, u32[]{:S(2)}) collective-permute-start(f32[512,64]{0,1:T(8,128)S(1)} %pad_maximum_fusion.3), channel_id=1, source_target_pairs={{5,0},{6,1},{7,2},{0,3},{1,4},{2,5},{3,6},{4,7},{13,8},{14,9},{15,... | collective-permute-start | bytes 393224 | tf_op jit(solution)/shard_map/ppermute | solution.py:16
  25.9 16.0 %collective-permute-start.24 = (f32[512,64]{0,1:T(8,128)S(1)}, f32[512,64]{0,1:T(8,128)S(1)}, u32[]{:S(2)}, u32[]{:S(2)}) collective-permute-start(f32[512,64]{0,1:T(8,128)S(1)} %pad_maximum_fusion.3), channel_id=1, source_target_pairs={{4,0},{5,1},{6,2},{7,3},{0,4},{1,5},{2,6},{3,7},{12,8},{13,9},{14,... | collective-permute-start | bytes 393224 | tf_op jit(solution)/shard_map/ppermute | solution.py:16
  27.9 14.1 %collective-permute-start.25 = (f32[512,64]{0,1:T(8,128)S(1)}, f32[512,64]{0,1:T(8,128)S(1)}, u32[]{:S(2)}, u32[]{:S(2)}) collective-permute-start(f32[512,64]{0,1:T(8,128)S(1)} %pad_maximum_fusion.3), channel_id=1, source_target_pairs={{3,0},{4,1},{5,2},{6,3},{7,4},{0,5},{1,6},{2,7},{11,8},{12,9},{13,... | collective-permute-start | bytes 393224 | tf_op jit(solution)/shard_map/ppermute | solution.py:16
  33.3 8.6 %collective-permute-start.26 = (f32[512,64]{0,1:T(8,128)S(1)}, f32[512,64]{0,1:T(8,128)S(1)}, u32[]{:S(2)}, u32[]{:S(2)}) collective-permute-start(f32[512,64]{0,1:T(8,128)S(1)} %pad_maximum_fusion.3), channel_id=1, source_target_pairs={{2,0},{3,1},{4,2},{5,3},{6,4},{7,5},{0,6},{1,7},{10,8},{11,9},{12,... | collective-permute-start | bytes 393224 | tf_op jit(solution)/shard_map/ppermute | solution.py:16
  36.7 8.0 %collective-permute-start.27 = (f32[512,64]{0,1:T(8,128)S(1)}, f32[512,64]{0,1:T(8,128)}, u32[]{:S(2)}, u32[]{:S(2)}) collective-permute-start(f32[512,64]{0,1:T(8,128)S(1)} %pad_maximum_fusion.3), channel_id=1, source_target_pairs={{1,0},{2,1},{3,2},{4,3},{5,4},{6,5},{7,6},{0,7},{9,8},{10,9},{11,1... | collective-permute-start | bytes 393224 | tf_op jit(solution)/shard_map/ppermute | solution.py:16
  41.9 4.4 %copy-start.4 = (f32[1,32,640]{2,1,0:T(8,128)S(1)}, f32[1,32,640]{2,1,0:T(8,128)}, u32[]{:S(2)}) copy-start(f32[1,32,640]{2,1,0:T(8,128)} %param.32) | copy-start | bytes 245764
  47.7 12.0 %collective-permute-start = (f32[32,2368]{1,0:T(8,128)S(1)}, f32[32,2368]{1,0:T(8,128)}, u32[]{:S(2)}, u32[]{:S(2)}) collective-permute-start(f32[32,2368]{1,0:T(8,128)S(1)} %param), channel_id=1, source_target_pairs={{1016,0},{0,8},{8,16},{16,24},{24,32},{32,40},{40,48},{48,56},{56,... | collective-permute-start | bytes 909320 | tf_op jit(solution)/shard_map/cond/branch_0_fun/ppermute | solution.py:16
  63.3 19.7 %collective-permute-start.28 = (f32[512,64]{0,1:T(8,128)}, f32[512,64]{0,1:T(8,128)S(1)}, u32[]{:S(2)}, u32[]{:S(2)}) collective-permute-start(f32[512,64]{0,1:T(8,128)} %pad_maximum_fusion.4), channel_id=1, source_target_pairs={{7,0},{0,1},{1,2},{2,3},{3,4},{4,5},{5,6},{6,7},{15,8},{8,9},{9,10... | collective-permute-start | bytes 393224 | tf_op jit(solution)/shard_map/ppermute | solution.py:16
  66.9 19.1 %collective-permute-start.29 = (f32[512,64]{0,1:T(8,128)}, f32[512,64]{0,1:T(8,128)S(1)}, u32[]{:S(2)}, u32[]{:S(2)}) collective-permute-start(f32[512,64]{0,1:T(8,128)} %pad_maximum_fusion.4), channel_id=1, source_target_pairs={{6,0},{7,1},{0,2},{1,3},{2,4},{3,5},{4,6},{5,7},{14,8},{15,9},{8,1... | collective-permute-start | bytes 393224 | tf_op jit(solution)/shard_map/ppermute | solution.py:16
  70.5 17.4 %collective-permute-start.30 = (f32[512,64]{0,1:T(8,128)}, f32[512,64]{0,1:T(8,128)S(1)}, u32[]{:S(2)}, u32[]{:S(2)}) collective-permute-start(f32[512,64]{0,1:T(8,128)} %pad_maximum_fusion.4), channel_id=1, source_target_pairs={{5,0},{6,1},{7,2},{0,3},{1,4},{2,5},{3,6},{4,7},{13,8},{14,9},{15,... | collective-permute-start | bytes 393224 | tf_op jit(solution)/shard_map/ppermute | solution.py:16
  73.8 14.2 %collective-permute-start.31 = (f32[512,64]{0,1:T(8,128)}, f32[512,64]{0,1:T(8,128)S(1)}, u32[]{:S(2)}, u32[]{:S(2)}) collective-permute-start(f32[512,64]{0,1:T(8,128)} %pad_maximum_fusion.4), channel_id=1, source_target_pairs={{4,0},{5,1},{6,2},{7,3},{0,4},{1,5},{2,6},{3,7},{12,8},{13,9},{14,... | collective-permute-start | bytes 393224 | tf_op jit(solution)/shard_map/ppermute | solution.py:16
  76.6 11.3 %collective-permute-start.32 = (f32[512,64]{0,1:T(8,128)}, f32[512,64]{0,1:T(8,128)S(1)}, u32[]{:S(2)}, u32[]{:S(2)}) collective-permute-start(f32[512,64]{0,1:T(8,128)} %pad_maximum_fusion.4), channel_id=1, source_target_pairs={{3,0},{4,1},{5,2},{6,3},{7,4},{0,5},{1,6},{2,7},{11,8},{12,9},{13,... | collective-permute-start | bytes 393224 | tf_op jit(solution)/shard_map/ppermute | solution.py:16
  83.0 7.1 %collective-permute-start.33 = (f32[512,64]{0,1:T(8,128)}, f32[512,64]{0,1:T(8,128)S(1)}, u32[]{:S(2)}, u32[]{:S(2)}) collective-permute-start(f32[512,64]{0,1:T(8,128)} %pad_maximum_fusion.4), channel_id=1, source_target_pairs={{2,0},{3,1},{4,2},{5,3},{6,4},{7,5},{0,6},{1,7},{10,8},{11,9},{12,... | collective-permute-start | bytes 393224 | tf_op jit(solution)/shard_map/ppermute | solution.py:16
  86.0 7.1 %collective-permute-start.34 = (f32[512,64]{0,1:T(8,128)}, f32[512,64]{0,1:T(8,128)S(1)}, u32[]{:S(2)}, u32[]{:S(2)}) collective-permute-start(f32[512,64]{0,1:T(8,128)} %pad_maximum_fusion.4), channel_id=1, source_target_pairs={{1,0},{2,1},{3,2},{4,3},{5,4},{6,5},{7,6},{0,7},{9,8},{10,9},{11,1... | collective-permute-start | bytes 393224 | tf_op jit(solution)/shard_map/ppermute | solution.py:16
  95.2 12.5 %collective-permute-start.8 = (f32[32,2368]{1,0:T(8,128)S(1)}, f32[32,2368]{1,0:T(8,128)}, u32[]{:S(2)}, u32[]{:S(2)}) collective-permute-start(f32[32,2368]{1,0:T(8,128)S(1)} %param.8), channel_id=1, source_target_pairs={{1008,0},{1016,8},{0,16},{8,24},{16,32},{24,40},{32,48},{40,56},{4... | collective-permute-start | bytes 909320 | tf_op jit(solution)/shard_map/cond/branch_1_fun/ppermute | solution.py:16
  111.2 17.6 %collective-permute-start.35 = (f32[512,64]{0,1:T(8,128)}, f32[512,64]{0,1:T(8,128)S(1)}, u32[]{:S(2)}, u32[]{:S(2)}) collective-permute-start(f32[512,64]{0,1:T(8,128)} %pad_maximum_fusion.5), channel_id=1, source_target_pairs={{7,0},{0,1},{1,2},{2,3},{3,4},{4,5},{5,6},{6,7},{15,8},{8,9},{9,10... | collective-permute-start | bytes 393224 | tf_op jit(solution)/shard_map/ppermute | solution.py:16
  113.7 19.6 %collective-permute-start.36 = (f32[512,64]{0,1:T(8,128)}, f32[512,64]{0,1:T(8,128)S(1)}, u32[]{:S(2)}, u32[]{:S(2)}) collective-permute-start(f32[512,64]{0,1:T(8,128)} %pad_maximum_fusion.5), channel_id=1, source_target_pairs={{6,0},{7,1},{0,2},{1,3},{2,4},{3,5},{4,6},{5,7},{14,8},{15,9},{8,1... | collective-permute-start | bytes 393224 | tf_op jit(solution)/shard_map/ppermute | solution.py:16
  117.5 18.4 %collective-permute-start.37 = (f32[512,64]{0,1:T(8,128)}, f32[512,64]{0,1:T(8,128)S(1)}, u32[]{:S(2)}, u32[]{:S(2)}) collective-permute-start(f32[512,64]{0,1:T(8,128)} %pad_maximum_fusion.5), channel_id=1, source_target_pairs={{5,0},{6,1},{7,2},{0,3},{1,4},{2,5},{3,6},{4,7},{13,8},{14,9},{15,... | collective-permute-start | bytes 393224 | tf_op jit(solution)/shard_map/ppermute | solution.py:16
  121.2 14.7 %collective-permute-start.38 = (f32[512,64]{0,1:T(8,128)}, f32[512,64]{0,1:T(8,128)S(1)}, u32[]{:S(2)}, u32[]{:S(2)}) collective-permute-start(f32[512,64]{0,1:T(8,128)} %pad_maximum_fusion.5), channel_id=1, source_target_pairs={{4,0},{5,1},{6,2},{7,3},{0,4},{1,5},{2,6},{3,7},{12,8},{13,9},{14,... | collective-permute-start | bytes 393224 | tf_op jit(solution)/shard_map/ppermute | solution.py:16
  124.1 11.8 %collective-permute-start.39 = (f32[512,64]{0,1:T(8,128)}, f32[512,64]{0,1:T(8,128)S(1)}, u32[]{:S(2)}, u32[]{:S(2)}) collective-permute-start(f32[512,64]{0,1:T(8,128)} %pad_maximum_fusion.5), channel_id=1, source_target_pairs={{3,0},{4,1},{5,2},{6,3},{7,4},{0,5},{1,6},{2,7},{11,8},{12,9},{13,... | collective-permute-start | bytes 393224 | tf_op jit(solution)/shard_map/ppermute | solution.py:16
  128.8 7.3 %collective-permute-start.40 = (f32[512,64]{0,1:T(8,128)}, f32[512,64]{0,1:T(8,128)S(1)}, u32[]{:S(2)}, u32[]{:S(2)}) collective-permute-start(f32[512,64]{0,1:T(8,128)} %pad_maximum_fusion.5), channel_id=1, source_target_pairs={{2,0},{3,1},{4,2},{5,3},{6,4},{7,5},{0,6},{1,7},{10,8},{11,9},{12,... | collective-permute-start | bytes 393224 | tf_op jit(solution)/shard_map/ppermute | solution.py:16
  133.3 7.2 %collective-permute-start.41 = (f32[512,64]{0,1:T(8,128)}, f32[512,64]{0,1:T(8,128)}, u32[]{:S(2)}, u32[]{:S(2)}) collective-permute-start(f32[512,64]{0,1:T(8,128)} %pad_maximum_fusion.5), channel_id=1, source_target_pairs={{1,0},{2,1},{3,2},{4,3},{5,4},{6,5},{7,6},{0,7},{9,8},{10,9},{11,1... | collective-permute-start | bytes 393224 | tf_op jit(solution)/shard_map/ppermute | solution.py:16
  143.5 10.1 %collective-permute-start.16 = (f32[32,2368]{1,0:T(8,128)S(1)}, f32[32,2368]{1,0:T(8,128)}, u32[]{:S(2)}, u32[]{:S(2)}) collective-permute-start(f32[32,2368]{1,0:T(8,128)S(1)} %param.16), channel_id=1, source_target_pairs={{992,0},{1000,8},{1008,16},{1016,24},{0,32},{8,40},{16,48},{24,56}... | collective-permute-start | bytes 909320 | tf_op jit(solution)/shard_map/cond/branch_2_fun/ppermute | solution.py:16

commit v2 on v1

--- a/solution.py
+++ b/solution.py
@@ -28,10 +28,13 @@
     return lax.switch(level, [make(bit) for bit in range(levels)], values)
 
 
-def fsdp_sum(part):
-    total = part
-    for distance in range(1, lax.axis_size("fsdp")):
-        total = total + shifted(part, "fsdp", distance)
+def fsdp_sum(total):
+    size = lax.axis_size("fsdp")
+    bit = 1
+    while bit < size:
+        route = [(i, i ^ bit) for i in range(size)]
+        total = total + lax.ppermute(total, "fsdp", route)
+        bit *= 2
     return total
 
 

time: 157 us -> 189 us (1.20)
  the two profiles are of different devices: /device:TPU:4 before, /device:TPU:2 now
where the time goes in v2:
time: 189 us; the launch traced here: 188 us
  waiting for transfers between devices  109 us (58%)
  starting transfers between devices  59.3 us (31%)
  matrix products  12.2 us (6%)
  other arithmetic  3.34 us (2%)
  local copies, waits for them, and re-layouts  2.82 us (1%)
    ppermute x3, waiting for transfers between devices, shifted(): return lax.ppermute(block, axis, route)  69.7 us
    ppermute x9, waiting for transfers between devices, fsdp_sum(): total = total + lax.ppermute(total, 'fsdp', route)  39.5 us
    ppermute x9, starting transfers between devices, fsdp_sum(): total = total + lax.ppermute(total, 'fsdp', route)  37.4 us
    ppermute x3, starting transfers between devices, shifted(): return lax.ppermute(block, axis, route)  21.9 us
    dot_general x6, matrix products, contract_rows(): lax.dot_general(left, right, (((1,), (1,)), ((), ())), preferred_element_...  6.36 us
    dot_general x6, matrix products, contract_tokens(): lax.dot_general(left, right, (((0,), (0,)), ((), ())), preferred_element_...  5.86 us
  transfers between devices with their start and end apart: 12, of which 12 were waited for; matrix products, arithmetic and copies ran while one was open for 0% of the time, Pallas kernels for 0%

profile of v2, /device:TPU:2, one launch (start us, length us, event | category | flops | bytes accessed | tf_op | source)
XLA Modules:
  0.0 188.5 jit_solution(12939029278038031269)
XLA Ops:
  0.6 0.0 copy-start
  0.6 0.0 copy-start.2
  0.7 1.5 copy-done
  2.1 0.0 copy-start.1
  2.1 0.0 copy-start.3
  2.1 1.4 fusion.9
  3.5 0.0 copy-done.2
  3.5 1.4 fusion.29
  4.9 3.5 %collective-permute-start.21 = (f32[512,64]{0,1:T(8,128)S(1)}, f32[512,64]{0,1:T(8,128)S(1)}, u32[]{:S(2)}, u32[]{:S(2)}) collective-permute-start(f32[512,64]{0,1:T(8,128)S(1)} %pad_maximum_fusion.3), channel_id=1, source_target_pairs={{0,1},{1,0},{2,3},{3,2},{4,5},{5,4},{6,7},{7,6},{8,9},{9,8},{10,11... | collective-permute-start | bytes 393224 | tf_op jit(solution)/shard_map/ppermute | solution.py:36
  8.4 3.6 %collective-permute-done.21 = f32[512,64]{0,1:T(8,128)S(1)} collective-permute-done((f32[512,64]{0,1:T(8,128)S(1)}, f32[512,64]{0,1:T(8,128)S(1)}, u32[]{:S(2)}, u32[]{:S(2)}) %collective-permute-start.21) | collective-permute-done | bytes 131104 | tf_op jit(solution)/shard_map/ppermute | solution.py:36
  12.1 0.0 copy-start.4
  12.1 15.0 %collective-permute-start.22 = (f32[512,64]{0,1:T(8,128)S(1)}, f32[512,64]{0,1:T(8,128)S(1)}, u32[]{:S(2)}, u32[]{:S(2)}) collective-permute-start(f32[512,64]{0,1:T(8,128)S(1)} %fusion.61), channel_id=1, source_target_pairs={{0,2},{1,3},{2,0},{3,1},{4,6},{5,7},{6,4},{7,5},{8,10},{9,11},{10,... | collective-permute-start | bytes 393224 | tf_op jit(solution)/shard_map/ppermute | solution.py:36
  27.1 2.9 %collective-permute-done.22 = f32[512,64]{0,1:T(8,128)S(1)} collective-permute-done((f32[512,64]{0,1:T(8,128)S(1)}, f32[512,64]{0,1:T(8,128)S(1)}, u32[]{:S(2)}, u32[]{:S(2)}) %collective-permute-start.22) | collective-permute-done | bytes 131104 | tf_op jit(solution)/shard_map/ppermute | solution.py:36
  30.0 1.9 %collective-permute-start.23 = (f32[512,64]{0,1:T(8,128)S(1)}, f32[512,64]{0,1:T(8,128)S(1)}, u32[]{:S(2)}, u32[]{:S(2)}) collective-permute-start(f32[512,64]{0,1:T(8,128)S(1)} %add.77), channel_id=1, source_target_pairs={{0,4},{1,5},{2,6},{3,7},{4,0},{5,1},{6,2},{7,3},{8,12},{9,13},{10,... | collective-permute-start | bytes 393224 | tf_op jit(solution)/shard_map/ppermute | solution.py:36
  32.6 5.8 %collective-permute-done.23 = f32[512,64]{0,1:T(8,128)S(1)} collective-permute-done((f32[512,64]{0,1:T(8,128)S(1)}, f32[512,64]{0,1:T(8,128)S(1)}, u32[]{:S(2)}, u32[]{:S(2)}) %collective-permute-start.23) | collective-permute-done | bytes 131104 | tf_op jit(solution)/shard_map/ppermute | solution.py:36
  38.4 0.0 copy-done.1
  38.4 0.0 copy-done.3
  38.4 0.6 bitcast_subtract_fusion
  39.1 0.0 copy-done.4
  39.1 1.3 bitcast_subtract_fusion.1
  40.4 38.4 %conditional.3 = (f32[32,2368]{1,0:T(8,128)}) conditional(s32[]{:T(128)} %clamp.9, f32[32,2368]{1,0:T(8,128)S(1)} %pad_maximum_fusion, f32[32,2368]{1,0:T(8,128)S(1)} %pad_maximum_fusion, f32[32,2368]{1,0:T(8,128)S(1)} %pad_maximum_fusion, f32[32,2368]{1,0:T(8,128)S(1)} %pad_maximum_fusion, ...), branch_computations={%region_0.1_spmd, %region_1.2_spmd, %region_2.3_spmd, %region_3.4_... | conditional | bytes 1212464 | solution.py:28
  40.5 18.1 %collective-permute-start.6 = (f32[32,2368]{1,0:T(8,128)S(1)}, f32[32,2368]{1,0:T(8,128)}, u32[]{:S(2)}, u32[]{:S(2)}) collective-permute-start(f32[32,2368]{1,0:T(8,128)S(1)} %param.6), channel_id=1, source_target_pairs={{512,0},{520,8},{528,16},{536,24},{544,32},{552,40},{560,48},{568,... | collective-permute-start | bytes 909320 | tf_op jit(solution)/shard_map/cond/branch_6_fun/ppermute | solution.py:16
  58.6 20.3 %collective-permute-done.6 = f32[32,2368]{1,0:T(8,128)} collective-permute-done((f32[32,2368]{1,0:T(8,128)S(1)}, f32[32,2368]{1,0:T(8,128)}, u32[]{:S(2)}, u32[]{:S(2)}) %collective-permute-start.6) | collective-permute-done | bytes 303136 | tf_op jit(solution)/shard_map/cond/branch_6_fun/ppermute | solution.py:16
  78.9 1.0 add_multiply_fusion.2
  79.9 1.4 fusion.26
  81.3 0.4 fusion.16
  81.7 2.0 %collective-permute-start.24 = (f32[512,64]{0,1:T(8,128)S(1)}, f32[512,64]{0,1:T(8,128)S(1)}, u32[]{:S(2)}, u32[]{:S(2)}) collective-permute-start(f32[512,64]{0,1:T(8,128)S(1)} %pad_maximum_fusion.4), channel_id=1, source_target_pairs={{0,1},{1,0},{2,3},{3,2},{4,5},{5,4},{6,7},{7,6},{8,9},{9,8},{10,11... | collective-permute-start | bytes 393224 | tf_op jit(solution)/shard_map/ppermute | solution.py:36
  83.7 4.8 %collective-permute-done.24 = f32[512,64]{0,1:T(8,128)S(1)} collective-permute-done((f32[512,64]{0,1:T(8,128)S(1)}, f32[512,64]{0,1:T(8,128)S(1)}, u32[]{:S(2)}, u32[]{:S(2)}) %collective-permute-start.24) | collective-permute-done | bytes 131104 | tf_op jit(solution)/shard_map/ppermute | solution.py:36
  88.6 4.0 %collective-permute-start.25 = (f32[512,64]{0,1:T(8,128)S(1)}, f32[512,64]{0,1:T(8,128)S(1)}, u32[]{:S(2)}, u32[]{:S(2)}) collective-permute-start(f32[512,64]{0,1:T(8,128)S(1)} %fusion.60), channel_id=1, source_target_pairs={{0,2},{1,3},{2,0},{3,1},{4,6},{5,7},{6,4},{7,5},{8,10},{9,11},{10,... | collective-permute-start | bytes 393224 | tf_op jit(solution)/shard_map/ppermute | solution.py:36
  92.6 2.9 %collective-permute-done.25 = f32[512,64]{0,1:T(8,128)S(1)} collective-permute-done((f32[512,64]{0,1:T(8,128)S(1)}, f32[512,64]{0,1:T(8,128)S(1)}, u32[]{:S(2)}, u32[]{:S(2)}) %collective-permute-start.25) | collective-permute-done | bytes 131104 | tf_op jit(solution)/shard_map/ppermute | solution.py:36
  95.5 1.9 %collective-permute-start.26 = (f32[512,64]{0,1:T(8,128)S(1)}, f32[512,64]{0,1:T(8,128)S(1)}, u32[]{:S(2)}, u32[]{:S(2)}) collective-permute-start(f32[512,64]{0,1:T(8,128)S(1)} %add.84), channel_id=1, source_target_pairs={{0,4},{1,5},{2,6},{3,7},{4,0},{5,1},{6,2},{7,3},{8,12},{9,13},{10,... | collective-permute-start | bytes 393224 | tf_op jit(solution)/shard_map/ppermute | solution.py:36
  97.5 6.4 %collective-permute-done.26 = f32[512,64]{0,1:T(8,128)S(1)} collective-permute-done((f32[512,64]{0,1:T(8,128)S(1)}, f32[512,64]{0,1:T(8,128)S(1)}, u32[]{:S(2)}, u32[]{:S(2)}) %collective-permute-start.26) | collective-permute-done | bytes 131104 | tf_op jit(solution)/shard_map/ppermute | solution.py:36
  103.9 1.3 multiply_subtract_fusion.1
  105.3 0.6 multiply_subtract_fusion
  105.9 38.8 %conditional.4 = (f32[32,2368]{1,0:T(8,128)}) conditional(s32[]{:T(128)} %clamp.10, f32[32,2368]{1,0:T(8,128)S(1)} %pad_maximum_fusion.1, f32[32,2368]{1,0:T(8,128)S(1)} %pad_maximum_fusion.1, f32[32,2368]{1,0:T(8,128)S(1)} %pad_maximum_fusion.1, f32[32,2368]{1,0:T(8,128)S(1)} %pad_maximum_fusion.1, ...), branch_computations={%region_7.8_spmd, %region_8.9_spmd, %region_9.10_spmd, %region_10.... | conditional | bytes 1212464 | solution.py:28
  105.9 1.9 %collective-permute-start.7 = (f32[32,2368]{1,0:T(8,128)S(1)}, f32[32,2368]{1,0:T(8,128)}, u32[]{:S(2)}, u32[]{:S(2)}) collective-permute-start(f32[32,2368]{1,0:T(8,128)S(1)} %param.7), channel_id=1, source_target_pairs={{1016,0},{0,8},{8,16},{16,24},{24,32},{32,40},{40,48},{48,56},{56,... | collective-permute-start | bytes 909320 | tf_op jit(solution)/shard_map/cond/branch_0_fun/ppermute | solution.py:16
  107.9 36.9 %collective-permute-done.7 = f32[32,2368]{1,0:T(8,128)} collective-permute-done((f32[32,2368]{1,0:T(8,128)S(1)}, f32[32,2368]{1,0:T(8,128)}, u32[]{:S(2)}, u32[]{:S(2)}) %collective-permute-start.7) | collective-permute-done | bytes 303136 | tf_op jit(solution)/shard_map/cond/branch_0_fun/ppermute | solution.py:16
  144.7 1.0 add_multiply_fusion.1
  145.7 1.4 fusion.23
  147.1 0.4 fusion.19
  147.6 2.6 %collective-permute-start.27 = (f32[512,64]{0,1:T(8,128)S(1)}, f32[512,64]{0,1:T(8,128)S(1)}, u32[]{:S(2)}, u32[]{:S(2)}) collective-permute-start(f32[512,64]{0,1:T(8,128)S(1)} %pad_maximum_fusion.5), channel_id=1, source_target_pairs={{0,1},{1,0},{2,3},{3,2},{4,5},{5,4},{6,7},{7,6},{8,9},{9,8},{10,11... | collective-permute-start | bytes 393224 | tf_op jit(solution)/shard_map/ppermute | solution.py:36
  150.2 4.3 %collective-permute-done.27 = f32[512,64]{0,1:T(8,128)S(1)} collective-permute-done((f32[512,64]{0,1:T(8,128)S(1)}, f32[512,64]{0,1:T(8,128)S(1)}, u32[]{:S(2)}, u32[]{:S(2)}) %collective-permute-start.27) | collective-permute-done | bytes 131104 | tf_op jit(solution)/shard_map/ppermute | solution.py:36
  154.5 2.5 %collective-permute-start.28 = (f32[512,64]{0,1:T(8,128)S(1)}, f32[512,64]{0,1:T(8,128)S(1)}, u32[]{:S(2)}, u32[]{:S(2)}) collective-permute-start(f32[512,64]{0,1:T(8,128)S(1)} %fusion.59), channel_id=1, source_target_pairs={{0,2},{1,3},{2,0},{3,1},{4,6},{5,7},{6,4},{7,5},{8,10},{9,11},{10,... | collective-permute-start | bytes 393224 | tf_op jit(solution)/shard_map/ppermute | solution.py:36
  156.9 4.4 %collective-permute-done.28 = f32[512,64]{0,1:T(8,128)S(1)} collective-permute-done((f32[512,64]{0,1:T(8,128)S(1)}, f32[512,64]{0,1:T(8,128)S(1)}, u32[]{:S(2)}, u32[]{:S(2)}) %collective-permute-start.28) | collective-permute-done | bytes 131104 | tf_op jit(solution)/shard_map/ppermute | solution.py:36
  161.3 4.1 %collective-permute-start.29 = (f32[512,64]{0,1:T(8,128)S(1)}, f32[512,64]{0,1:T(8,128)S(1)}, u32[]{:S(2)}, u32[]{:S(2)}) collective-permute-start(f32[512,64]{0,1:T(8,128)S(1)} %add.92), channel_id=1, source_target_pairs={{0,4},{1,5},{2,6},{3,7},{4,0},{5,1},{6,2},{7,3},{8,12},{9,13},{10,... | collective-permute-start | bytes 393224 | tf_op jit(solution)/shard_map/ppermute | solution.py:36
  165.4 4.3 %collective-permute-done.29 = f32[512,64]{0,1:T(8,128)S(1)} collective-permute-done((f32[512,64]{0,1:T(8,128)S(1)}, f32[512,64]{0,1:T(8,128)S(1)}, u32[]{:S(2)}, u32[]{:S(2)}) %collective-permute-start.29) | collective-permute-done | bytes 131104 | tf_op jit(solution)/shard_map/ppermute | solution.py:36
  169.7 1.3 fusion.13
  171.1 0.6 fusion.1
  171.7 14.4 %conditional.5 = (f32[32,2368]{1,0:T(8,128)}) conditional(s32[]{:T(128)} %clamp.11, f32[32,2368]{1,0:T(8,128)S(1)} %pad_maximum_fusion.2, f32[32,2368]{1,0:T(8,128)S(1)} %pad_maximum_fusion.2, f32[32,2368]{1,0:T(8,128)S(1)} %pad_maximum_fusion.2, f32[32,2368]{1,0:T(8,128)S(1)} %pad_maximum_fusion.2, ...), branch_computations={%region_14.15_spmd, %region_15.16_spmd, %region_16.17_spmd, %regio... | conditional | bytes 1212464 | solution.py:28
  171.7 1.9 %collective-permute-start.15 = (f32[32,2368]{1,0:T(8,128)S(1)}, f32[32,2368]{1,0:T(8,128)}, u32[]{:S(2)}, u32[]{:S(2)}) collective-permute-start(f32[32,2368]{1,0:T(8,128)S(1)} %param.15), channel_id=1, source_target_pairs={{1008,0},{1016,8},{0,16},{8,24},{16,32},{24,40},{32,48},{40,56},{4... | collective-permute-start | bytes 909320 | tf_op jit(solution)/shard_map/cond/branch_1_fun/ppermute | solution.py:16
  173.7 12.5 %collective-permute-done.15 = f32[32,2368]{1,0:T(8,128)} collective-permute-done((f32[32,2368]{1,0:T(8,128)S(1)}, f32[32,2368]{1,0:T(8,128)}, u32[]{:S(2)}, u32[]{:S(2)}) %collective-permute-start.15) | collective-permute-done | bytes 303136 | tf_op jit(solution)/shard_map/cond/branch_1_fun/ppermute | solution.py:16
  186.1 1.0 add_multiply_fusion
  187.1 0.7 slice_bitcast_fusion
  187.8 0.6 slice_bitcast_fusion.1
  (15 shorter events, 0.3 us)
Async XLA Ops:
  0.6 1.5 copy-start
  0.6 2.9 %copy-start.2 = (f32[1,32,640]{2,1,0:T(8,128)S(1)}, f32[1,32,640]{2,1,0:T(8,128)}, u32[]{:S(2)}) copy-start(f32[1,32,640]{2,1,0:T(8,128)} %param.30) | copy-start | bytes 245764
  2.1 36.3 %copy-start.1 = (f32[1,32,1728]{2,1,0:T(8,128)S(1)}, f32[1,32,1728]{2,1,0:T(8,128)}, u32[]{:S(2)}) copy-start(f32[1,32,1728]{2,1,0:T(8,128)} %param.31) | copy-start | bytes 663556
  2.1 36.3 %copy-start.3 = (f32[1,32,1728]{2,1,0:T(8,128)S(1)}, f32[1,32,1728]{2,1,0:T(8,128)}, u32[]{:S(2)}) copy-start(f32[1,32,1728]{2,1,0:T(8,128)} %param.33) | copy-start | bytes 663556
  4.9 7.1 %collective-permute-start.21 = (f32[512,64]{0,1:T(8,128)S(1)}, f32[512,64]{0,1:T(8,128)S(1)}, u32[]{:S(2)}, u32[]{:S(2)}) collective-permute-start(f32[512,64]{0,1:T(8,128)S(1)} %pad_maximum_fusion.3), channel_id=1, source_target_pairs={{0,1},{1,0},{2,3},{3,2},{4,5},{5,4},{6,7},{7,6},{8,9},{9,8},{10,11... | collective-permute-start | bytes 393224 | tf_op jit(solution)/shard_map/ppermute | solution.py:36
  12.1 27.0 %copy-start.4 = (f32[1,32,640]{2,1,0:T(8,128)S(1)}, f32[1,32,640]{2,1,0:T(8,128)}, u32[]{:S(2)}) copy-start(f32[1,32,640]{2,1,0:T(8,128)} %param.32) | copy-start | bytes 245764
  12.1 17.9 %collective-permute-start.22 = (f32[512,64]{0,1:T(8,128)S(1)}, f32[512,64]{0,1:T(8,128)S(1)}, u32[]{:S(2)}, u32[]{:S(2)}) collective-permute-start(f32[512,64]{0,1:T(8,128)S(1)} %fusion.61), channel_id=1, source_target_pairs={{0,2},{1,3},{2,0},{3,1},{4,6},{5,7},{6,4},{7,5},{8,10},{9,11},{10,... | collective-permute-start | bytes 393224 | tf_op jit(solution)/shard_map/ppermute | solution.py:36
  30.0 8.4 %collective-permute-start.23 = (f32[512,64]{0,1:T(8,128)S(1)}, f32[512,64]{0,1:T(8,128)S(1)}, u32[]{:S(2)}, u32[]{:S(2)}) collective-permute-start(f32[512,64]{0,1:T(8,128)S(1)} %add.77), channel_id=1, source_target_pairs={{0,4},{1,5},{2,6},{3,7},{4,0},{5,1},{6,2},{7,3},{8,12},{9,13},{10,... | collective-permute-start | bytes 393224 | tf_op jit(solution)/shard_map/ppermute | solution.py:36
  40.5 38.4 %collective-permute-start.6 = (f32[32,2368]{1,0:T(8,128)S(1)}, f32[32,2368]{1,0:T(8,128)}, u32[]{:S(2)}, u32[]{:S(2)}) collective-permute-start(f32[32,2368]{1,0:T(8,128)S(1)} %param.6), channel_id=1, source_target_pairs={{512,0},{520,8},{528,16},{536,24},{544,32},{552,40},{560,48},{568,... | collective-permute-start | bytes 909320 | tf_op jit(solution)/shard_map/cond/branch_6_fun/ppermute | solution.py:16
  81.7 6.9 %collective-permute-start.24 = (f32[512,64]{0,1:T(8,128)S(1)}, f32[512,64]{0,1:T(8,128)S(1)}, u32[]{:S(2)}, u32[]{:S(2)}) collective-permute-start(f32[512,64]{0,1:T(8,128)S(1)} %pad_maximum_fusion.4), channel_id=1, source_target_pairs={{0,1},{1,0},{2,3},{3,2},{4,5},{5,4},{6,7},{7,6},{8,9},{9,8},{10,11... | collective-permute-start | bytes 393224 | tf_op jit(solution)/shard_map/ppermute | solution.py:36
  88.6 6.9 %collective-permute-start.25 = (f32[512,64]{0,1:T(8,128)S(1)}, f32[512,64]{0,1:T(8,128)S(1)}, u32[]{:S(2)}, u32[]{:S(2)}) collective-permute-start(f32[512,64]{0,1:T(8,128)S(1)} %fusion.60), channel_id=1, source_target_pairs={{0,2},{1,3},{2,0},{3,1},{4,6},{5,7},{6,4},{7,5},{8,10},{9,11},{10,... | collective-permute-start | bytes 393224 | tf_op jit(solution)/shard_map/ppermute | solution.py:36
  95.5 8.4 %collective-permute-start.26 = (f32[512,64]{0,1:T(8,128)S(1)}, f32[512,64]{0,1:T(8,128)S(1)}, u32[]{:S(2)}, u32[]{:S(2)}) collective-permute-start(f32[512,64]{0,1:T(8,128)S(1)} %add.84), channel_id=1, source_target_pairs={{0,4},{1,5},{2,6},{3,7},{4,0},{5,1},{6,2},{7,3},{8,12},{9,13},{10,... | collective-permute-start | bytes 393224 | tf_op jit(solution)/shard_map/ppermute | solution.py:36
  105.9 38.8 %collective-permute-start.7 = (f32[32,2368]{1,0:T(8,128)S(1)}, f32[32,2368]{1,0:T(8,128)}, u32[]{:S(2)}, u32[]{:S(2)}) collective-permute-start(f32[32,2368]{1,0:T(8,128)S(1)} %param.7), channel_id=1, source_target_pairs={{1016,0},{0,8},{8,16},{16,24},{24,32},{32,40},{40,48},{48,56},{56,... | collective-permute-start | bytes 909320 | tf_op jit(solution)/shard_map/cond/branch_0_fun/ppermute | solution.py:16
  147.6 6.9 %collective-permute-start.27 = (f32[512,64]{0,1:T(8,128)S(1)}, f32[512,64]{0,1:T(8,128)S(1)}, u32[]{:S(2)}, u32[]{:S(2)}) collective-permute-start(f32[512,64]{0,1:T(8,128)S(1)} %pad_maximum_fusion.5), channel_id=1, source_target_pairs={{0,1},{1,0},{2,3},{3,2},{4,5},{5,4},{6,7},{7,6},{8,9},{9,8},{10,11... | collective-permute-start | bytes 393224 | tf_op jit(solution)/shard_map/ppermute | solution.py:36
  154.5 6.9 %collective-permute-start.28 = (f32[512,64]{0,1:T(8,128)S(1)}, f32[512,64]{0,1:T(8,128)S(1)}, u32[]{:S(2)}, u32[]{:S(2)}) collective-permute-start(f32[512,64]{0,1:T(8,128)S(1)} %fusion.59), channel_id=1, source_target_pairs={{0,2},{1,3},{2,0},{3,1},{4,6},{5,7},{6,4},{7,5},{8,10},{9,11},{10,... | collective-permute-start | bytes 393224 | tf_op jit(solution)/shard_map/ppermute | solution.py:36
  161.3 8.4 %collective-permute-start.29 = (f32[512,64]{0,1:T(8,128)S(1)}, f32[512,64]{0,1:T(8,128)S(1)}, u32[]{:S(2)}, u32[]{:S(2)}) collective-permute-start(f32[512,64]{0,1:T(8,128)S(1)} %add.92), channel_id=1, source_target_pairs={{0,4},{1,5},{2,6},{3,7},{4,0},{5,1},{6,2},{7,3},{8,12},{9,13},{10,... | collective-permute-start | bytes 393224 | tf_op jit(solution)/shard_map/ppermute | solution.py:36
  171.7 14.4 %collective-permute-start.15 = (f32[32,2368]{1,0:T(8,128)S(1)}, f32[32,2368]{1,0:T(8,128)}, u32[]{:S(2)}, u32[]{:S(2)}) collective-permute-start(f32[32,2368]{1,0:T(8,128)S(1)} %param.15), channel_id=1, source_target_pairs={{1008,0},{1016,8},{0,16},{8,24},{16,32},{24,40},{32,48},{40,56},{4... | collective-permute-start | bytes 909320 | tf_op jit(solution)/shard_map/cond/branch_1_fun/ppermute | solution.py:16

commit v3 on v2

--- a/solution.py
+++ b/solution.py
@@ -33,7 +33,8 @@
     bit = 1
     while bit < size:
         route = [(i, i ^ bit) for i in range(size)]
-        total = total + lax.ppermute(total, "fsdp", route)
+        sent = lax.ppermute(total.astype(jnp.bfloat16), "fsdp", route)
+        total = total + sent.astype(jnp.float32)
         bit *= 2
     return total
 
@@ -79,7 +80,8 @@
         stepped = jnp.concatenate(
             [factor_a - learn_rate * moment_da, factor_b - learn_rate * moment_db], axis=1
         )
-        merged = 0.5 * (stepped + partner_after(stepped, level, levels))
+        received = partner_after(stepped.astype(jnp.bfloat16), level, levels)
+        merged = 0.5 * (stepped + received.astype(jnp.float32))
         factor_a = merged[:, :own_width]
         factor_b = merged[:, own_width:]
     return (factor_a[None], factor_b[None])

time: 189 us -> 129 us (0.68)
  the two profiles are of different devices: /device:TPU:2 before, /device:TPU:10 now
where the time goes in v3:
time: 129 us; the launch traced here: 128 us
  waiting for transfers between devices  67.3 us (52%)
  starting transfers between devices  40.5 us (31%)
  matrix products  12.2 us (9%)
  other arithmetic  3.19 us (2%)
  local copies, waits for them, and re-layouts  2.82 us (2%)
  between operations  1.6 us (1%)
    ppermute x9, starting transfers between devices, fsdp_sum(): sent = lax.ppermute(total.astype(jnp.bfloat16), 'fsdp', route)  34.7 us
    ppermute x9, waiting for transfers between devices, fsdp_sum(): sent = lax.ppermute(total.astype(jnp.bfloat16), 'fsdp', route)  34.7 us
    ppermute x3, waiting for transfers between devices, shifted(): return lax.ppermute(block, axis, route)  32.6 us
    dot_general x6, matrix products, contract_rows(): lax.dot_general(left, right, (((1,), (1,)), ((), ())), preferred_element_...  6.35 us
    dot_general x6, matrix products, contract_tokens(): lax.dot_general(left, right, (((0,), (0,)), ((), ())), preferred_element_...  5.86 us
    ppermute x3, starting transfers between devices, shifted(): return lax.ppermute(block, axis, route)  5.76 us
    mul x3, other arithmetic, shards(): merged = 0.5 * (stepped + received.astype(jnp.float32))  2.84 us
  transfers between devices with their start and end apart: 12, of which 12 were waited for; matrix products, arithmetic and copies ran while one was open for 0% of the time, Pallas kernels for 0%

profile of v3, /device:TPU:10, one launch (start us, length us, event | category | flops | bytes accessed | tf_op | source)
XLA Modules:
  0.0 127.7 jit_solution(15942246466804634881)
XLA Ops:
  0.6 0.0 copy-start
  0.6 0.0 copy-start.2
  0.7 1.5 %copy-done = bf16[1,512,1728]{1,2,0:T(8,128)(2,1)S(1)} copy-done((bf16[1,512,1728]{1,2,0:T(8,128)(2,1)S(1)}, bf16[1,512,1728]{1,2,0:T(8,128)(2,1)}, u32[]{:S(2)}) %copy-start) | copy-done | bytes 1769496
  2.1 0.0 copy-start.1
  2.1 0.0 copy-start.3
  2.1 1.4 %fusion.9 = f32[512,32]{0,1:T(8,128)S(1)} fusion(bf16[1,512,1728]{1,2,0:T(8,128)(2,1)S(1)} %copy-done, f32[1,32,1728]{2,1,0:T(8,128)} %param.31), kind=kOutput, calls=%fused_computation.12 | convolution fusion | flops 56678400 | bytes 2056192 | tf_op jit(solution)/shard_map/dot_general | solution.py:43
  3.5 0.0 copy-done.2
  3.5 1.4 %fusion.29 = f32[512,32]{0,1:T(8,128)S(1)} fusion(bf16[1,512,5120]{2,1,0:T(8,128)(2,1)} %param.28, s32[]{:T(128)S(6)} %select_n.18, f32[1,32,640]{2,1,0:T(8,128)S(1)} %copy-done.2), kind=kOutput, calls=%fused_computation.31 | convolution fusion | flops 20992000 | bytes 802820 | tf_op jit(solution)/shard_map/dot_general | solution.py:43
  4.9 2.4 %collective-permute-start.21 = (bf16[512,64]{0,1:T(8,128)(2,1)S(1)}, bf16[512,64]{0,1:T(8,128)(2,1)S(1)}, u32[]{:S(2)}, u32[]{:S(2)}) collective-permute-start(bf16[512,64]{0,1:T(8,128)(2,1)S(1)} %fusion.44), channel_id=1, source_target_pairs={{0,1},{1,0},{2,3},{3,2},{4,5},{5,4},{6,7},{7,6},{8,9},{9,8},{10,11... | collective-permute-start | bytes 196616 | tf_op jit(solution)/shard_map/ppermute | solution.py:36
  7.3 3.8 %collective-permute-done.21 = bf16[512,64]{0,1:T(8,128)(2,1)S(1)} collective-permute-done((bf16[512,64]{0,1:T(8,128)(2,1)S(1)}, bf16[512,64]{0,1:T(8,128)(2,1)S(1)}, u32[]{:S(2)}, u32[]{:S(2)}) %collective-permute-start.21) | collective-permute-done | bytes 65568 | tf_op jit(solution)/shard_map/ppermute | solution.py:36
  11.1 0.0 copy-start.4
  11.1 13.7 %collective-permute-start.22 = (bf16[512,64]{0,1:T(8,128)(2,1)S(1)}, bf16[512,64]{0,1:T(8,128)(2,1)S(1)}, u32[]{:S(2)}, u32[]{:S(2)}) collective-permute-start(bf16[512,64]{0,1:T(8,128)(2,1)S(1)} %fusion.59), channel_id=1, source_target_pairs={{0,2},{1,3},{2,0},{3,1},{4,6},{5,7},{6,4},{7,5},{8,10},{9,11},{10,... | collective-permute-start | bytes 196616 | tf_op jit(solution)/shard_map/ppermute | solution.py:36
  24.8 2.2 %collective-permute-done.22 = bf16[512,64]{0,1:T(8,128)(2,1)S(1)} collective-permute-done((bf16[512,64]{0,1:T(8,128)(2,1)S(1)}, bf16[512,64]{0,1:T(8,128)(2,1)S(1)}, u32[]{:S(2)}, u32[]{:S(2)}) %collective-permute-start.22) | collective-permute-done | bytes 65568 | tf_op jit(solution)/shard_map/ppermute | solution.py:36
  27.1 1.9 %collective-permute-start.23 = (bf16[512,64]{0,1:T(8,128)(2,1)S(1)}, bf16[512,64]{0,1:T(8,128)(2,1)S(1)}, u32[]{:S(2)}, u32[]{:S(2)}) collective-permute-start(bf16[512,64]{0,1:T(8,128)(2,1)S(1)} %fusion.45), channel_id=1, source_target_pairs={{0,4},{1,5},{2,6},{3,7},{4,0},{5,1},{6,2},{7,3},{8,12},{9,13},{10,... | collective-permute-start | bytes 196616 | tf_op jit(solution)/shard_map/ppermute | solution.py:36
  29.7 5.1 %collective-permute-done.23 = bf16[512,64]{0,1:T(8,128)(2,1)S(1)} collective-permute-done((bf16[512,64]{0,1:T(8,128)(2,1)S(1)}, bf16[512,64]{0,1:T(8,128)(2,1)S(1)}, u32[]{:S(2)}, u32[]{:S(2)}) %collective-permute-start.23) | collective-permute-done | bytes 65568 | tf_op jit(solution)/shard_map/ppermute | solution.py:36
  34.8 0.0 copy-done.1
  34.8 0.0 copy-done.3
  34.8 0.6 bitcast_subtract_fusion
  35.4 0.0 copy-done.4
  35.4 1.3 %bitcast_subtract_fusion.1 = (f32[32,640]{1,0:T(8,128)S(1)}, f32[32,640]{1,0:T(8,128)S(1)}) fusion(f32[1,32,640]{2,1,0:T(8,128)S(1)} %copy-done.2, bf16[1,512,5120]{2,1,0:T(8,128)(2,1)} %param.28, s32[]{:T(128)S(6)} %select_n.18, f32[512,64]{0,1:T(8,128)S(1)} %convert_add_fusion.6, f32[1,32,640]{2,1,0:T(8,128)S(1)} %copy-done.4), kind=kOutput, calls=%fused_computation.74 | convolution fusion | flops 21073920 | bytes 1015812 | tf_op jit(solution)/shard_map/dot_general | solution.py:49
  36.8 12.4 %conditional.12 = (bf16[32,2368]{1,0:T(8,128)(2,1)}) conditional(s32[]{:T(128)} %clamp.9, bf16[32,2368]{1,0:T(8,128)(2,1)S(1)} %fusion.39, bf16[32,2368]{1,0:T(8,128)(2,1)S(1)} %fusion.39, bf16[32,2368]{1,0:T(8,128)(2,1)S(1)} %fusion.39, bf16[32,2368]{1,0:T(8,128)(2,1)S(1)} %fusion.39, ...), branch_computations={%region_0.1_spmd, %region_1.2_spmd, %region_2.3_spmd, %region_3.4_... | conditional | bytes 606256
  36.8 1.9 %collective-permute-start.2 = (bf16[32,2368]{1,0:T(8,128)(2,1)S(1)}, bf16[32,2368]{1,0:T(8,128)(2,1)}, u32[]{:S(2)}, u32[]{:S(2)}) collective-permute-start(bf16[32,2368]{1,0:T(8,128)(2,1)S(1)} %param.2), channel_id=1, source_target_pairs={{992,0},{1000,8},{1008,16},{1016,24},{0,32},{8,40},{16,48},{24,56}... | collective-permute-start | bytes 454664 | tf_op jit(solution)/shard_map/cond/branch_2_fun/ppermute | solution.py:16
  38.7 10.4 %collective-permute-done.2 = bf16[32,2368]{1,0:T(8,128)(2,1)} collective-permute-done((bf16[32,2368]{1,0:T(8,128)(2,1)S(1)}, bf16[32,2368]{1,0:T(8,128)(2,1)}, u32[]{:S(2)}, u32[]{:S(2)}) %collective-permute-start.2) | collective-permute-done | bytes 151584 | tf_op jit(solution)/shard_map/cond/branch_2_fun/ppermute | solution.py:16
  49.2 0.9 add_multiply_fusion.2
  50.1 0.4 fusion.16
  50.5 1.4 %fusion.26 = f32[512,32]{0,1:T(8,128)S(1)} fusion(bf16[1,512,5120]{2,1,0:T(8,128)(2,1)} %param.28, s32[]{:T(128)S(6)} %select_n.18, f32[32,2368]{1,0:T(8,128)S(1)} %add_multiply_fusion.2), kind=kOutput, calls=%fused_computation.28 | convolution fusion | flops 20971520 | bytes 761860 | tf_op jit(solution)/shard_map/dot_general | solution.py:43
  52.0 2.4 %collective-permute-start.24 = (bf16[512,64]{0,1:T(8,128)(2,1)S(1)}, bf16[512,64]{0,1:T(8,128)(2,1)S(1)}, u32[]{:S(2)}, u32[]{:S(2)}) collective-permute-start(bf16[512,64]{0,1:T(8,128)(2,1)S(1)} %fusion.43), channel_id=1, source_target_pairs={{0,1},{1,0},{2,3},{3,2},{4,5},{5,4},{6,7},{7,6},{8,9},{9,8},{10,11... | collective-permute-start | bytes 196616 | tf_op jit(solution)/shard_map/ppermute | solution.py:36
  54.3 3.8 %collective-permute-done.24 = bf16[512,64]{0,1:T(8,128)(2,1)S(1)} collective-permute-done((bf16[512,64]{0,1:T(8,128)(2,1)S(1)}, bf16[512,64]{0,1:T(8,128)(2,1)S(1)}, u32[]{:S(2)}, u32[]{:S(2)}) %collective-permute-start.24) | collective-permute-done | bytes 65568 | tf_op jit(solution)/shard_map/ppermute | solution.py:36
  58.1 2.4 %collective-permute-start.25 = (bf16[512,64]{0,1:T(8,128)(2,1)S(1)}, bf16[512,64]{0,1:T(8,128)(2,1)S(1)}, u32[]{:S(2)}, u32[]{:S(2)}) collective-permute-start(bf16[512,64]{0,1:T(8,128)(2,1)S(1)} %fusion.60), channel_id=1, source_target_pairs={{0,2},{1,3},{2,0},{3,1},{4,6},{5,7},{6,4},{7,5},{8,10},{9,11},{10,... | collective-permute-start | bytes 196616 | tf_op jit(solution)/shard_map/ppermute | solution.py:36
  60.6 4.1 %collective-permute-done.25 = bf16[512,64]{0,1:T(8,128)(2,1)S(1)} collective-permute-done((bf16[512,64]{0,1:T(8,128)(2,1)S(1)}, bf16[512,64]{0,1:T(8,128)(2,1)S(1)}, u32[]{:S(2)}, u32[]{:S(2)}) %collective-permute-start.25) | collective-permute-done | bytes 65568 | tf_op jit(solution)/shard_map/ppermute | solution.py:36
  64.8 3.6 %collective-permute-start.26 = (bf16[512,64]{0,1:T(8,128)(2,1)S(1)}, bf16[512,64]{0,1:T(8,128)(2,1)S(1)}, u32[]{:S(2)}, u32[]{:S(2)}) collective-permute-start(bf16[512,64]{0,1:T(8,128)(2,1)S(1)} %fusion.46), channel_id=1, source_target_pairs={{0,4},{1,5},{2,6},{3,7},{4,0},{5,1},{6,2},{7,3},{8,12},{9,13},{10,... | collective-permute-start | bytes 196616 | tf_op jit(solution)/shard_map/ppermute | solution.py:36
  68.4 4.0 %collective-permute-done.26 = bf16[512,64]{0,1:T(8,128)(2,1)S(1)} collective-permute-done((bf16[512,64]{0,1:T(8,128)(2,1)S(1)}, bf16[512,64]{0,1:T(8,128)(2,1)S(1)}, u32[]{:S(2)}, u32[]{:S(2)}) %collective-permute-start.26) | collective-permute-done | bytes 65568 | tf_op jit(solution)/shard_map/ppermute | solution.py:36
  72.5 0.6 multiply_subtract_fusion
  73.1 1.3 %multiply_subtract_fusion.1 = (f32[32,640]{1,0:T(8,128)S(1)}, f32[32,640]{1,0:T(8,128)S(1)}) fusion(f32[32,2368]{1,0:T(8,128)S(1)} %add_multiply_fusion.2, bf16[1,512,5120]{2,1,0:T(8,128)(2,1)} %param.28, s32[]{:T(128)S(6)} %select_n.18, f32[512,64]{0,1:T(8,128)S(1)} %convert_add_fusion.3, f32[32,640]{1,0:T(8,128)S(1)} %get-tuple-element.68), kind=kOutput, calls=%fused_computation.75 | convolution fusion | flops 21073920 | bytes 1015812 | tf_op jit(solution)/shard_map/dot_general | solution.py:49
  74.5 9.9 %conditional.13 = (bf16[32,2368]{1,0:T(8,128)(2,1)}) conditional(s32[]{:T(128)} %clamp.10, bf16[32,2368]{1,0:T(8,128)(2,1)S(1)} %fusion.38, bf16[32,2368]{1,0:T(8,128)(2,1)S(1)} %fusion.38, bf16[32,2368]{1,0:T(8,128)(2,1)S(1)} %fusion.38, bf16[32,2368]{1,0:T(8,128)(2,1)S(1)} %fusion.38, ...), branch_computations={%region_7.8_spmd, %region_8.9_spmd, %region_9.10_spmd, %region_10.... | conditional | bytes 606256
  74.5 1.9 %collective-permute-start.10 = (bf16[32,2368]{1,0:T(8,128)(2,1)S(1)}, bf16[32,2368]{1,0:T(8,128)(2,1)}, u32[]{:S(2)}, u32[]{:S(2)}) collective-permute-start(bf16[32,2368]{1,0:T(8,128)(2,1)S(1)} %param.10), channel_id=1, source_target_pairs={{960,0},{968,8},{976,16},{984,24},{992,32},{1000,40},{1008,48},{10... | collective-permute-start | bytes 454664 | tf_op jit(solution)/shard_map/cond/branch_3_fun/ppermute | solution.py:16
  76.4 8.0 %collective-permute-done.10 = bf16[32,2368]{1,0:T(8,128)(2,1)} collective-permute-done((bf16[32,2368]{1,0:T(8,128)(2,1)S(1)}, bf16[32,2368]{1,0:T(8,128)(2,1)}, u32[]{:S(2)}, u32[]{:S(2)}) %collective-permute-start.10) | collective-permute-done | bytes 151584 | tf_op jit(solution)/shard_map/cond/branch_3_fun/ppermute | solution.py:16
  84.4 0.9 add_multiply_fusion.1
  85.3 0.4 fusion.19
  85.7 1.4 %fusion.23 = f32[512,32]{0,1:T(8,128)S(1)} fusion(bf16[1,512,5120]{2,1,0:T(8,128)(2,1)} %param.28, s32[]{:T(128)S(6)} %select_n.18, f32[32,2368]{1,0:T(8,128)S(1)} %add_multiply_fusion.1), kind=kOutput, calls=%fused_computation.25 | convolution fusion | flops 20971520 | bytes 761860 | tf_op jit(solution)/shard_map/dot_general | solution.py:43
  87.1 2.4 %collective-permute-start.27 = (bf16[512,64]{0,1:T(8,128)(2,1)S(1)}, bf16[512,64]{0,1:T(8,128)(2,1)S(1)}, u32[]{:S(2)}, u32[]{:S(2)}) collective-permute-start(bf16[512,64]{0,1:T(8,128)(2,1)S(1)} %fusion.42), channel_id=1, source_target_pairs={{0,1},{1,0},{2,3},{3,2},{4,5},{5,4},{6,7},{7,6},{8,9},{9,8},{10,11... | collective-permute-start | bytes 196616 | tf_op jit(solution)/shard_map/ppermute | solution.py:36
  89.5 3.8 %collective-permute-done.27 = bf16[512,64]{0,1:T(8,128)(2,1)S(1)} collective-permute-done((bf16[512,64]{0,1:T(8,128)(2,1)S(1)}, bf16[512,64]{0,1:T(8,128)(2,1)S(1)}, u32[]{:S(2)}, u32[]{:S(2)}) %collective-permute-start.27) | collective-permute-done | bytes 65568 | tf_op jit(solution)/shard_map/ppermute | solution.py:36
  93.3 2.4 %collective-permute-start.28 = (bf16[512,64]{0,1:T(8,128)(2,1)S(1)}, bf16[512,64]{0,1:T(8,128)(2,1)S(1)}, u32[]{:S(2)}, u32[]{:S(2)}) collective-permute-start(bf16[512,64]{0,1:T(8,128)(2,1)S(1)} %fusion.61), channel_id=1, source_target_pairs={{0,2},{1,3},{2,0},{3,1},{4,6},{5,7},{6,4},{7,5},{8,10},{9,11},{10,... | collective-permute-start | bytes 196616 | tf_op jit(solution)/shard_map/ppermute | solution.py:36
  95.7 3.8 %collective-permute-done.28 = bf16[512,64]{0,1:T(8,128)(2,1)S(1)} collective-permute-done((bf16[512,64]{0,1:T(8,128)(2,1)S(1)}, bf16[512,64]{0,1:T(8,128)(2,1)S(1)}, u32[]{:S(2)}, u32[]{:S(2)}) %collective-permute-start.28) | collective-permute-done | bytes 65568 | tf_op jit(solution)/shard_map/ppermute | solution.py:36
  99.5 3.6 %collective-permute-start.29 = (bf16[512,64]{0,1:T(8,128)(2,1)S(1)}, bf16[512,64]{0,1:T(8,128)(2,1)S(1)}, u32[]{:S(2)}, u32[]{:S(2)}) collective-permute-start(bf16[512,64]{0,1:T(8,128)(2,1)S(1)} %fusion.47), channel_id=1, source_target_pairs={{0,4},{1,5},{2,6},{3,7},{4,0},{5,1},{6,2},{7,3},{8,12},{9,13},{10,... | collective-permute-start | bytes 196616 | tf_op jit(solution)/shard_map/ppermute | solution.py:36
  103.1 4.0 %collective-permute-done.29 = bf16[512,64]{0,1:T(8,128)(2,1)S(1)} collective-permute-done((bf16[512,64]{0,1:T(8,128)(2,1)S(1)}, bf16[512,64]{0,1:T(8,128)(2,1)S(1)}, u32[]{:S(2)}, u32[]{:S(2)}) %collective-permute-start.29) | collective-permute-done | bytes 65568 | tf_op jit(solution)/shard_map/ppermute | solution.py:36
  107.2 0.6 fusion.1
  107.8 1.3 %fusion.13 = f32[32,640]{1,0:T(8,128)S(1)} fusion(bf16[1,512,5120]{2,1,0:T(8,128)(2,1)} %param.28, s32[]{:T(128)S(6)} %select_n.18, f32[32,640]{1,0:T(8,128)S(1)} %get-tuple-element.72, f32[32,2368]{1,0:T(8,128)S(1)} %add_multiply_fusion.1, f32[512,64]{0,1:T(8,128)S(1)} %convert_add_fusion), kind=kOutput, calls=%fused_computation.17 | convolution fusion | flops 21073920 | bytes 933892 | tf_op jit(solution)/shard_map/dot_general | solution.py:49
  109.2 16.2 %conditional.14 = (bf16[32,2368]{1,0:T(8,128)(2,1)}) conditional(s32[]{:T(128)} %clamp.11, bf16[32,2368]{1,0:T(8,128)(2,1)S(1)} %fusion.37, bf16[32,2368]{1,0:T(8,128)(2,1)S(1)} %fusion.37, bf16[32,2368]{1,0:T(8,128)(2,1)S(1)} %fusion.37, bf16[32,2368]{1,0:T(8,128)(2,1)S(1)} %fusion.37, ...), branch_computations={%region_14.15_spmd, %region_15.16_spmd, %region_16.17_spmd, %regio... | conditional | bytes 606256
  109.2 1.9 %collective-permute-start.18 = (bf16[32,2368]{1,0:T(8,128)(2,1)S(1)}, bf16[32,2368]{1,0:T(8,128)(2,1)}, u32[]{:S(2)}, u32[]{:S(2)}) collective-permute-start(bf16[32,2368]{1,0:T(8,128)(2,1)S(1)} %param.18), channel_id=1, source_target_pairs={{896,0},{904,8},{912,16},{920,24},{928,32},{936,40},{944,48},{952,... | collective-permute-start | bytes 454664 | tf_op jit(solution)/shard_map/cond/branch_4_fun/ppermute | solution.py:16
  111.2 14.2 %collective-permute-done.18 = bf16[32,2368]{1,0:T(8,128)(2,1)} collective-permute-done((bf16[32,2368]{1,0:T(8,128)(2,1)S(1)}, bf16[32,2368]{1,0:T(8,128)(2,1)}, u32[]{:S(2)}, u32[]{:S(2)}) %collective-permute-start.18) | collective-permute-done | bytes 151584 | tf_op jit(solution)/shard_map/cond/branch_4_fun/ppermute | solution.py:16
  125.4 0.9 add_multiply_fusion
  126.3 0.6 slice_bitcast_fusion.1
  127.0 0.7 slice_bitcast_fusion
  (15 shorter events, 0.4 us)
Async XLA Ops:
  0.6 1.5 %copy-start = (bf16[1,512,1728]{1,2,0:T(8,128)(2,1)S(1)}, bf16[1,512,1728]{1,2,0:T(8,128)(2,1)}, u32[]{:S(2)}) copy-start(bf16[1,512,1728]{1,2,0:T(8,128)(2,1)} %param.29) | copy-start | bytes 5308420
  0.6 2.9 %copy-start.2 = (f32[1,32,640]{2,1,0:T(8,128)S(1)}, f32[1,32,640]{2,1,0:T(8,128)}, u32[]{:S(2)}) copy-start(f32[1,32,640]{2,1,0:T(8,128)} %param.30) | copy-start | bytes 245764
  2.1 32.6 %copy-start.1 = (f32[1,32,1728]{2,1,0:T(8,128)S(1)}, f32[1,32,1728]{2,1,0:T(8,128)}, u32[]{:S(2)}) copy-start(f32[1,32,1728]{2,1,0:T(8,128)} %param.31) | copy-start | bytes 663556
  2.1 32.7 %copy-start.3 = (f32[1,32,1728]{2,1,0:T(8,128)S(1)}, f32[1,32,1728]{2,1,0:T(8,128)}, u32[]{:S(2)}) copy-start(f32[1,32,1728]{2,1,0:T(8,128)} %param.33) | copy-start | bytes 663556
  4.9 6.2 %collective-permute-start.21 = (bf16[512,64]{0,1:T(8,128)(2,1)S(1)}, bf16[512,64]{0,1:T(8,128)(2,1)S(1)}, u32[]{:S(2)}, u32[]{:S(2)}) collective-permute-start(bf16[512,64]{0,1:T(8,128)(2,1)S(1)} %fusion.44), channel_id=1, source_target_pairs={{0,1},{1,0},{2,3},{3,2},{4,5},{5,4},{6,7},{7,6},{8,9},{9,8},{10,11... | collective-permute-start | bytes 196616 | tf_op jit(solution)/shard_map/ppermute | solution.py:36
  11.1 24.3 %copy-start.4 = (f32[1,32,640]{2,1,0:T(8,128)S(1)}, f32[1,32,640]{2,1,0:T(8,128)}, u32[]{:S(2)}) copy-start(f32[1,32,640]{2,1,0:T(8,128)} %param.32) | copy-start | bytes 245764
  11.1 15.9 %collective-permute-start.22 = (bf16[512,64]{0,1:T(8,128)(2,1)S(1)}, bf16[512,64]{0,1:T(8,128)(2,1)S(1)}, u32[]{:S(2)}, u32[]{:S(2)}) collective-permute-start(bf16[512,64]{0,1:T(8,128)(2,1)S(1)} %fusion.59), channel_id=1, source_target_pairs={{0,2},{1,3},{2,0},{3,1},{4,6},{5,7},{6,4},{7,5},{8,10},{9,11},{10,... | collective-permute-start | bytes 196616 | tf_op jit(solution)/shard_map/ppermute | solution.py:36
  27.1 7.7 %collective-permute-start.23 = (bf16[512,64]{0,1:T(8,128)(2,1)S(1)}, bf16[512,64]{0,1:T(8,128)(2,1)S(1)}, u32[]{:S(2)}, u32[]{:S(2)}) collective-permute-start(bf16[512,64]{0,1:T(8,128)(2,1)S(1)} %fusion.45), channel_id=1, source_target_pairs={{0,4},{1,5},{2,6},{3,7},{4,0},{5,1},{6,2},{7,3},{8,12},{9,13},{10,... | collective-permute-start | bytes 196616 | tf_op jit(solution)/shard_map/ppermute | solution.py:36
  36.8 12.4 %collective-permute-start.2 = (bf16[32,2368]{1,0:T(8,128)(2,1)S(1)}, bf16[32,2368]{1,0:T(8,128)(2,1)}, u32[]{:S(2)}, u32[]{:S(2)}) collective-permute-start(bf16[32,2368]{1,0:T(8,128)(2,1)S(1)} %param.2), channel_id=1, source_target_pairs={{992,0},{1000,8},{1008,16},{1016,24},{0,32},{8,40},{16,48},{24,56}... | collective-permute-start | bytes 454664 | tf_op jit(solution)/shard_map/cond/branch_2_fun/ppermute | solution.py:16
  52.0 6.2 %collective-permute-start.24 = (bf16[512,64]{0,1:T(8,128)(2,1)S(1)}, bf16[512,64]{0,1:T(8,128)(2,1)S(1)}, u32[]{:S(2)}, u32[]{:S(2)}) collective-permute-start(bf16[512,64]{0,1:T(8,128)(2,1)S(1)} %fusion.43), channel_id=1, source_target_pairs={{0,1},{1,0},{2,3},{3,2},{4,5},{5,4},{6,7},{7,6},{8,9},{9,8},{10,11... | collective-permute-start | bytes 196616 | tf_op jit(solution)/shard_map/ppermute | solution.py:36
  58.1 6.6 %collective-permute-start.25 = (bf16[512,64]{0,1:T(8,128)(2,1)S(1)}, bf16[512,64]{0,1:T(8,128)(2,1)S(1)}, u32[]{:S(2)}, u32[]{:S(2)}) collective-permute-start(bf16[512,64]{0,1:T(8,128)(2,1)S(1)} %fusion.60), channel_id=1, source_target_pairs={{0,2},{1,3},{2,0},{3,1},{4,6},{5,7},{6,4},{7,5},{8,10},{9,11},{10,... | collective-permute-start | bytes 196616 | tf_op jit(solution)/shard_map/ppermute | solution.py:36
  64.8 7.7 %collective-permute-start.26 = (bf16[512,64]{0,1:T(8,128)(2,1)S(1)}, bf16[512,64]{0,1:T(8,128)(2,1)S(1)}, u32[]{:S(2)}, u32[]{:S(2)}) collective-permute-start(bf16[512,64]{0,1:T(8,128)(2,1)S(1)} %fusion.46), channel_id=1, source_target_pairs={{0,4},{1,5},{2,6},{3,7},{4,0},{5,1},{6,2},{7,3},{8,12},{9,13},{10,... | collective-permute-start | bytes 196616 | tf_op jit(solution)/shard_map/ppermute | solution.py:36
  74.5 9.9 %collective-permute-start.10 = (bf16[32,2368]{1,0:T(8,128)(2,1)S(1)}, bf16[32,2368]{1,0:T(8,128)(2,1)}, u32[]{:S(2)}, u32[]{:S(2)}) collective-permute-start(bf16[32,2368]{1,0:T(8,128)(2,1)S(1)} %param.10), channel_id=1, source_target_pairs={{960,0},{968,8},{976,16},{984,24},{992,32},{1000,40},{1008,48},{10... | collective-permute-start | bytes 454664 | tf_op jit(solution)/shard_map/cond/branch_3_fun/ppermute | solution.py:16
  87.1 6.2 %collective-permute-start.27 = (bf16[512,64]{0,1:T(8,128)(2,1)S(1)}, bf16[512,64]{0,1:T(8,128)(2,1)S(1)}, u32[]{:S(2)}, u32[]{:S(2)}) collective-permute-start(bf16[512,64]{0,1:T(8,128)(2,1)S(1)} %fusion.42), channel_id=1, source_target_pairs={{0,1},{1,0},{2,3},{3,2},{4,5},{5,4},{6,7},{7,6},{8,9},{9,8},{10,11... | collective-permute-start | bytes 196616 | tf_op jit(solution)/shard_map/ppermute | solution.py:36
  93.3 6.2 %collective-permute-start.28 = (bf16[512,64]{0,1:T(8,128)(2,1)S(1)}, bf16[512,64]{0,1:T(8,128)(2,1)S(1)}, u32[]{:S(2)}, u32[]{:S(2)}) collective-permute-start(bf16[512,64]{0,1:T(8,128)(2,1)S(1)} %fusion.61), channel_id=1, source_target_pairs={{0,2},{1,3},{2,0},{3,1},{4,6},{5,7},{6,4},{7,5},{8,10},{9,11},{10,... | collective-permute-start | bytes 196616 | tf_op jit(solution)/shard_map/ppermute | solution.py:36
  99.5 7.7 %collective-permute-start.29 = (bf16[512,64]{0,1:T(8,128)(2,1)S(1)}, bf16[512,64]{0,1:T(8,128)(2,1)S(1)}, u32[]{:S(2)}, u32[]{:S(2)}) collective-permute-start(bf16[512,64]{0,1:T(8,128)(2,1)S(1)} %fusion.47), channel_id=1, source_target_pairs={{0,4},{1,5},{2,6},{3,7},{4,0},{5,1},{6,2},{7,3},{8,12},{9,13},{10,... | collective-permute-start | bytes 196616 | tf_op jit(solution)/shard_map/ppermute | solution.py:36
  109.2 16.1 %collective-permute-start.18 = (bf16[32,2368]{1,0:T(8,128)(2,1)S(1)}, bf16[32,2368]{1,0:T(8,128)(2,1)}, u32[]{:S(2)}, u32[]{:S(2)}) collective-permute-start(bf16[32,2368]{1,0:T(8,128)(2,1)S(1)} %param.18), channel_id=1, source_target_pairs={{896,0},{904,8},{912,16},{920,24},{928,32},{936,40},{944,48},{952,... | collective-permute-start | bytes 454664 | tf_op jit(solution)/shard_map/cond/branch_4_fun/ppermute | solution.py:16
